TPU v7x, 256 devices: a whole 4x4x8 slice. The times are simulated.
256 devices in a mesh: pipe: 4 (over z_hi), dp: 64 (over y, x, z_lo, core).
Axes of the slice: x: 4, y: 4, z: 8 (z_hi: 4, z_lo: 2; z = z_hi * 2 + z_lo), core: 2. Of those that a mesh axis runs over, the one named last changes fastest.
Arguments:
- acts_in: bfloat16 [2, 4096, 4096], P(None, 'dp'), may hold values from -40 to 40
- cotangent: bfloat16 [2, 4096, 4096], P(None, 'dp'), may hold values from -6 to 6
- norm_gains: float32 [4, 4096], P('pipe'), may hold values from 0.1 to 1.9
- weights: bfloat16 [4, 256, 128, 128], P('pipe', 'dp'), may hold values from -0.1875 to 0.1875
- tile_columns: int32 [4, 256], P('pipe'), may hold values from 0 to 31, as said below
- lengths: int32 [2, 64], P(None, 'dp'), may hold values from 16 to 64
Outputs:
- section_out: bfloat16 [4, 2, 4096, 4096], P('pipe', None, 'dp')
- input_grad: bfloat16 [4, 2, 4096, 4096], P('pipe', None, 'dp')
- weight_grad: float32 [4, 256, 128, 128], P('pipe', 'dp')
Inputs may be any that keep to these rules, and one draw needn't show every extreme that they name: `tile_columns`: the 8 entries of one block row of a section (positions r * 8 to r * 8 + 7) are distinct.
All inputs are finite; a program needn't handle non-finite values.
Results may differ from a plain program's by a relative error of at most 0.0081.
Values may be sent and summed in bfloat16 or wider, within the bound.
No kernel may reach another device: no remote copies, remote signals or barrier semaphores. Data moves between devices by JAX's collectives and lax.ppermute only.
A program may use at most 384 MiB of HBM per device.

v0:
```python
import jax
import jax.numpy as jnp
from jax import lax
from jax.sharding import PartitionSpec as P

TILE = 128
KEEP = 8


epsilon = 1e-05


def from_behind(value, axis, steps):
    count = lax.axis_size(axis)
    leading, last = (max(0, -steps), min(count, count - steps))
    return lax.ppermute(value, axis, [(source, source + steps) for source in range(leading, last)])


def normalize(section_input, section_gain):
    values = section_input.astype(jnp.float32)
    inv_rms = lax.rsqrt(jnp.mean(values * values, axis=-1, keepdims=True) + epsilon)
    unit_rows = values * inv_rms
    return (values, inv_rms, unit_rows, (unit_rows * section_gain).astype(jnp.bfloat16))


def sparse_product(hidden, tile_grid, column_flat):
    row_count = hidden.shape[0]
    blocks = tile_grid.shape[0]
    keep_count = tile_grid.shape[1]
    tile_parts = jnp.einsum(
        "trk,rjkn->trjn",
        hidden.reshape(row_count, blocks, TILE),
        tile_grid,
        preferred_element_type=jnp.float32,
    )
    placed = jnp.zeros((row_count, blocks, TILE), jnp.float32)
    placed = placed.at[:, column_flat, :].add(
        tile_parts.reshape(row_count, blocks * keep_count, TILE)
    )
    return placed.reshape(row_count, blocks * TILE)


def store_slot(buffer_all, new_value, micro_slot, is_live):
    old_value = lax.dynamic_index_in_dim(buffer_all, micro_slot, 0, keepdims=False)
    chosen = jnp.where(is_live, new_value, old_value)
    return lax.dynamic_update_index_in_dim(buffer_all, chosen, micro_slot, 0)


def on_device(acts_in, cotangent, norm_gains, weights, tile_columns, lengths):
    micro_count, row_count, model_width = acts_in.shape
    section_count = lax.axis_size("pipe")
    section_here = lax.axis_index("pipe")
    blocks = model_width // TILE
    section_gain = norm_gains[0]
    column_list = tile_columns[0]
    column_table = column_list.reshape(blocks, KEEP)
    gathered = lax.all_gather(weights[0], "dp", axis=0, tiled=True)
    tile_grid = gathered.reshape(blocks, KEEP, TILE, TILE)
    within = jnp.arange(row_count, dtype=jnp.int32)
    valid_rows = (within[None, :] < lengths).astype(jnp.float32)
    received = jnp.zeros((row_count, model_width), jnp.bfloat16)
    section_out = jnp.zeros_like(acts_in)
    saved_inputs = jnp.zeros_like(acts_in)

    def run_forward(section_input):
        values, inv_rms, unit_rows, hidden = normalize(section_input, section_gain)
        pre_act = sparse_product(hidden, tile_grid, column_list)
        return ((values + jax.nn.silu(pre_act)).astype(jnp.bfloat16), pre_act)

    def skip_forward(section_input):
        return (section_input, jnp.zeros((row_count, model_width), jnp.float32))

    for clock_tick in range(micro_count + section_count - 1):
        micro_index = clock_tick - section_here
        is_live = jnp.logical_and(micro_index >= 0, micro_index < micro_count)
        micro_slot = jnp.clip(micro_index, 0, micro_count - 1)
        first_input = lax.dynamic_index_in_dim(acts_in, micro_slot, 0, keepdims=False)
        section_input = jnp.where(section_here == 0, first_input, received)
        section_result, pre_act = lax.cond(is_live, run_forward, skip_forward, section_input)
        section_out = store_slot(section_out, section_result, micro_slot, is_live)
        saved_inputs = store_slot(saved_inputs, section_input, micro_slot, is_live)
        received = from_behind(section_result, "pipe", 1)

    def run_backward(section_input, grad_input, pre_input):
        values, inv_rms, unit_rows, hidden = normalize(section_input, section_gain)
        pre_act = sparse_product(hidden, tile_grid, column_list)
        sigmoid_part = jax.nn.sigmoid(pre_act)
        grad_float = grad_input.astype(jnp.float32)
        pre_delta = (grad_float * sigmoid_part * (1.0 + pre_act * (1.0 - sigmoid_part))).astype(
            jnp.bfloat16
        )
        picked = jnp.take(pre_delta.reshape(row_count, blocks, TILE), column_table, axis=1)
        hidden_delta = jnp.einsum(
            "trjn,rjkn->trk", picked, tile_grid, preferred_element_type=jnp.float32
        ).reshape(row_count, model_width)
        gained = hidden_delta * section_gain
        input_delta = grad_float + inv_rms * (
            gained - unit_rows * jnp.mean(gained * unit_rows, axis=-1, keepdims=True)
        )
        tile_term = jnp.einsum(
            "trk,trjn->rjkn",
            hidden.reshape(row_count, blocks, TILE),
            picked,
            preferred_element_type=jnp.float32,
        )
        return (input_delta.astype(jnp.bfloat16), hidden, pre_delta, tile_term)

    def skip_backward(section_input, grad_input, pre_input):
        tile_term = jnp.zeros((blocks, KEEP, TILE, TILE), jnp.float32)
        return (grad_input, jnp.zeros_like(grad_input), jnp.zeros_like(grad_input), tile_term)

    received = jnp.zeros((row_count, model_width), jnp.bfloat16)
    input_grad = jnp.zeros_like(acts_in)
    tile_grads = jnp.zeros((blocks, KEEP, TILE, TILE), jnp.float32)
    for clock_tick in range(micro_count + section_count - 1):
        micro_index = clock_tick - (section_count - 1 - section_here)
        is_live = jnp.logical_and(micro_index >= 0, micro_index < micro_count)
        micro_slot = jnp.clip(micro_index, 0, micro_count - 1)
        last_cot = lax.dynamic_index_in_dim(cotangent, micro_slot, 0, keepdims=False).astype(
            jnp.float32
        )
        last_mask = lax.dynamic_index_in_dim(valid_rows, micro_slot, 0, keepdims=False)
        last_grad = (last_cot * last_mask[:, None]).astype(jnp.bfloat16)
        grad_input = jnp.where(section_here == section_count - 1, last_grad, received)
        section_input = lax.dynamic_index_in_dim(saved_inputs, micro_slot, 0, keepdims=False)
        pre_input = jnp.zeros((), jnp.float32)
        input_delta, hidden, pre_delta, tile_term = lax.cond(
            is_live, run_backward, skip_backward, section_input, grad_input, pre_input
        )
        input_grad = store_slot(input_grad, input_delta, micro_slot, is_live)
        tile_grads = tile_grads + tile_term
        received = from_behind(input_delta, "pipe", -1)
    weight_grad = lax.psum_scatter(
        tile_grads.reshape(blocks * KEEP, TILE, TILE), "dp", scatter_dimension=0, tiled=True
    )
    return (section_out[None], input_grad[None], weight_grad[None])


def solution(mesh):
    placed = (
        P(None, "dp", None),
        P(None, "dp", None),
        P("pipe", None),
        P("pipe", "dp", None, None),
        P("pipe", None),
        P(None, "dp"),
    )
    return jax.shard_map(
        on_device,
        mesh=mesh,
        in_specs=placed,
        out_specs=(
            P("pipe", None, "dp", None),
            P("pipe", None, "dp", None),
            P("pipe", "dp", None, None),
        ),
        check_vma=False,
    )
```

profile of v0, /device:TPU:64, one launch (start us, length us, event | category | flops | bytes accessed | tf_op | source)
XLA Modules:
  0.0 1068.6 jit_solution(10068926407569655386)
XLA Ops:
  8.1 1.2 select_dynamic-update-slice_fusion
  9.3 115.6 %all-gather.3.cloned.1.call-done = bf16[1,256,128,128]{3,2,0,1:T(8,128)(2,1)} async-done(((bf16[1,4,128,128]{3,2,0,1:T(8,128)(2,1)}), bf16[1,256,128,128]{3,2,0,1:T(8,128)(2,1)}) %all-gather.3.cloned.1.call-update) | async-done | bytes 8388624 | tf_op jit(solution)/shard_map/all_gather | solution.py:57
  124.8 5.1 collective-permute-start
  130.0 45.5 %collective-permute-done = bf16[64,4096]{1,0:T(8,128)(2,1)S(1)} collective-permute-done((bf16[64,4096]{1,0:T(8,128)(2,1)S(1)}, bf16[64,4096]{1,0:T(8,128)(2,1)S(1)}, u32[]{:S(2)}, u32[]{:S(2)}) %collective-permute-start) | collective-permute-done | bytes 524320 | tf_op jit(solution)/shard_map/ppermute | solution.py:16
  175.5 1.3 bitcast_dynamic-update-slice_fusion.8
  176.8 36.6 %conditional.11 = (bf16[64,4096]{1,0:T(8,128)(2,1)S(1)}) conditional(s32[]{:T(128)} %convert_element_type.289, bf16[64,4096]{1,0:T(8,128)(2,1)S(1)} %get-tuple-element.306, (bf16[64,4096]{1,0:T(8,128)(2,1)S(1)}, s32[256]{0:T(256)}, f32[1,4096]{1,0:T(1,128)}, bf16[32,8,128,128]{3,2,1,0:T(8,128)(2,1)}) %tuple.152), branch_computations={%region_4.5_spmd, %region_5.8_spmd} | conditional | flops 542638912 | bytes 48254988 | solution.py:79
  177.7 0.9 fusion.17
  178.7 8.0 fusion.18
  186.9 26.1 %scatter_fusion.1 = f32[64,32,128]{2,0,1:T(8,128)S(1)} fusion(f32[64,32,128]{2,0,1:T(8,128)S(1)} %broadcast.417, s32[256]{0:T(256)S(1)} %compare_select_fusion.1, f32[256,64,128]{2,1,0:T(8,128)} %bitcast.720), kind=kCustom, calls=%fused_computation.6 | custom fusion | flops 2097152 | bytes 25166848 | tf_op jit(solution)/shard_map/cond/branch_1_fun/scatter-add | solution.py:37
  213.4 1.9 collective-permute-start.1
  215.4 14.2 %collective-permute-done.1 = bf16[64,4096]{1,0:T(8,128)(2,1)S(1)} collective-permute-done((bf16[64,4096]{1,0:T(8,128)(2,1)S(1)}, bf16[64,4096]{1,0:T(8,128)(2,1)S(1)}, u32[]{:S(2)}, u32[]{:S(2)}) %collective-permute-start.1) | collective-permute-done | bytes 524320 | tf_op jit(solution)/shard_map/ppermute | solution.py:16
  229.6 1.3 bitcast_dynamic-update-slice_fusion.7
  230.9 36.6 %conditional.12 = (bf16[64,4096]{1,0:T(8,128)(2,1)S(1)}) conditional(s32[]{:T(128)} %convert_element_type.290, bf16[64,4096]{1,0:T(8,128)(2,1)S(1)} %get-tuple-element.304, (bf16[64,4096]{1,0:T(8,128)(2,1)S(1)}, s32[256]{0:T(256)}, f32[1,4096]{1,0:T(1,128)}, bf16[32,8,128,128]{3,2,1,0:T(8,128)(2,1)}) %tuple.153), branch_computations={%region_8.9_spmd, %region_9.12_spmd} | conditional | flops 542638912 | bytes 48254988 | solution.py:79
  231.9 0.9 fusion.27
  232.9 8.0 fusion.28
  241.0 26.1 %scatter_fusion.2 = f32[64,32,128]{2,0,1:T(8,128)S(1)} fusion(f32[64,32,128]{2,0,1:T(8,128)S(1)} %broadcast.422, s32[256]{0:T(256)S(1)} %compare_select_fusion.2, f32[256,64,128]{2,1,0:T(8,128)} %bitcast.721), kind=kCustom, calls=%fused_computation.7 | custom fusion | flops 2097152 | bytes 25166848 | tf_op jit(solution)/shard_map/cond/branch_1_fun/scatter-add | solution.py:37
  267.5 3.4 collective-permute-start.2
  271.5 11.3 %collective-permute-done.2 = bf16[64,4096]{1,0:T(8,128)(2,1)S(1)} collective-permute-done((bf16[64,4096]{1,0:T(8,128)(2,1)S(1)}, bf16[64,4096]{1,0:T(8,128)(2,1)S(1)}, u32[]{:S(2)}, u32[]{:S(2)}) %collective-permute-start.2) | collective-permute-done | bytes 524320 | tf_op jit(solution)/shard_map/ppermute | solution.py:16
  282.8 1.3 bitcast_dynamic-update-slice_fusion.6
  284.4 41.4 %collective-permute-start.3 = (bf16[64,4096]{1,0:T(8,128)(2,1)S(1)}, bf16[64,4096]{1,0:T(8,128)(2,1)S(1)}, u32[]{:S(2)}, u32[]{:S(2)}) collective-permute-start(bf16[64,4096]{1,0:T(8,128)(2,1)S(1)} %get-tuple-element.349), channel_id=1, source_target_pairs={{0,64},{64,128},{128,192},{1,65},{65,129},{129,193},{2,66},{66,130... | collective-permute-start | bytes 1572872 | tf_op jit(solution)/shard_map/ppermute | solution.py:16
  325.8 2.0 fusion.190
  328.3 1.3 reduce.8
  329.8 5.4 collective-permute-done.3
  335.2 2.1 bitcast_dynamic-update-slice_fusion.5
  337.3 7.9 conditional.15
  337.3 7.9 broadcast.437
  345.2 1.9 collective-permute-start.4
  347.1 14.2 %collective-permute-done.4 = bf16[64,4096]{1,0:T(8,128)(2,1)S(1)} collective-permute-done((bf16[64,4096]{1,0:T(8,128)(2,1)}, bf16[64,4096]{1,0:T(8,128)(2,1)S(1)}, u32[]{:S(2)}, u32[]{:S(2)}) %collective-permute-start.4) | collective-permute-done | bytes 524320 | tf_op jit(solution)/shard_map/ppermute | solution.py:16
  361.3 1.3 fusion.191
  362.6 8.2 conditional.16
  362.6 7.8 broadcast.444
  370.8 1.9 collective-permute-start.5
  372.7 105.6 %collective-permute-done.5 = bf16[64,4096]{1,0:T(8,128)(2,1)S(1)} collective-permute-done((bf16[64,4096]{1,0:T(8,128)(2,1)S(1)}, bf16[64,4096]{1,0:T(8,128)(2,1)S(1)}, u32[]{:S(2)}, u32[]{:S(2)}) %collective-permute-start.5) | collective-permute-done | bytes 524320 | tf_op jit(solution)/shard_map/ppermute | solution.py:16
  478.4 2.1 fusion.192
  480.4 58.4 %conditional.17 = (bf16[64,4096]{1,0:T(8,128)(2,1)}, f32[32,8,128,128]{2,3,1,0:T(8,128)}) conditional(s32[]{:T(128)} %convert_element_type.302, bf16[64,4096]{1,0:T(8,128)(2,1)} %fusion.192, (bf16[64,4096]{1,0:T(8,128)(2,1)}, bf16[2,64,4096]{2,1,0:T(8,128)(2,1)S(1)}, s32[]{:T(128)}, s32[256]{0:T(256)S(1)}, f32[1,4096]{1,0:T(1,128)}, ...), branch_computations={%region_30.32_spmd, %region_31.36_spmd} | conditional | flops 1625559040 | bytes 123356808 | solution.py:127
  481.2 9.0 fusion.127
  490.4 26.1 %scatter_fusion.7 = f32[64,32,128]{2,0,1:T(8,128)S(1)} fusion(f32[64,32,128]{2,0,1:T(8,128)S(1)} %broadcast.455, s32[256]{0:T(256)S(1)} %compare_select_fusion.10, f32[256,64,128]{2,1,0:T(8,128)} %bitcast.716), kind=kCustom, calls=%fused_computation.12 | custom fusion | flops 2097152 | bytes 25166848 | tf_op jit(solution)/shard_map/cond/branch_1_fun/scatter-add | solution.py:37
  516.6 1.5 copy_bitcast_fusion.2
  518.0 3.0 gather_fusion.2
  521.1 8.0 fusion.123
  529.1 2.2 fusion.113
  531.3 7.5 convolution_bitcast_fusion.2
  538.9 1.9 collective-permute-start.6
  540.8 12.5 %collective-permute-done.6 = bf16[64,4096]{1,0:T(8,128)(2,1)S(1)} collective-permute-done((bf16[64,4096]{1,0:T(8,128)(2,1)}, bf16[64,4096]{1,0:T(8,128)(2,1)S(1)}, u32[]{:S(2)}, u32[]{:S(2)}) %collective-permute-start.6) | collective-permute-done | bytes 524320 | tf_op jit(solution)/shard_map/ppermute | solution.py:16
  553.3 1.3 fusion.193
  554.5 55.8 %conditional.18 = (bf16[64,4096]{1,0:T(8,128)(2,1)S(1)}, f32[32,8,128,128]{2,3,1,0:T(8,128)}) conditional(s32[]{:T(128)} %convert_element_type.306, bf16[64,4096]{1,0:T(8,128)(2,1)S(1)} %fusion.193, (bf16[64,4096]{1,0:T(8,128)(2,1)S(1)}, bf16[2,64,4096]{2,1,0:T(8,128)(2,1)S(1)}, s32[]{:T(128)}, s32[256]{0:T(256)S(1)}, f32[1,4096]{1,0:T(1,128)}, ...), branch_computations={%region_35.37_spmd, %region_36.41_spmd} | conditional | flops 1625559040 | bytes 123356808 | solution.py:127
  555.4 9.0 fusion.154
  564.6 26.1 %scatter_fusion.8 = f32[64,32,128]{2,0,1:T(8,128)S(1)} fusion(f32[64,32,128]{2,0,1:T(8,128)S(1)} %broadcast.462, s32[256]{0:T(256)S(1)} %compare_select_fusion.12, f32[256,64,128]{2,1,0:T(8,128)} %bitcast.717), kind=kCustom, calls=%fused_computation.13 | custom fusion | flops 2097152 | bytes 25166848 | tf_op jit(solution)/shard_map/cond/branch_1_fun/scatter-add | solution.py:37
  591.2 3.0 gather_fusion.3
  594.2 8.0 fusion.150
  602.6 7.7 convolution_bitcast_fusion.3
  610.3 1.9 collective-permute-start.7
  612.2 11.4 %collective-permute-done.7 = bf16[64,4096]{1,0:T(8,128)(2,1)S(1)} collective-permute-done((bf16[64,4096]{1,0:T(8,128)(2,1)S(1)}, bf16[64,4096]{1,0:T(8,128)(2,1)S(1)}, u32[]{:S(2)}, u32[]{:S(2)}) %collective-permute-start.7) | collective-permute-done | bytes 524320 | tf_op jit(solution)/shard_map/ppermute | solution.py:16
  623.6 1.3 fusion.194
  624.9 8.2 conditional.19
  624.9 7.9 broadcast.465
  633.1 34.7 %add_add_fusion = f32[32,8,128,128]{2,3,1,0:T(8,128)} fusion(f32[32,8,128,128]{2,3,1,0:T(8,128)} %get-tuple-element.298, f32[32,8,128,128]{2,3,1,0:T(8,128)} %get-tuple-element.297, f32[32,8,128,128]{2,3,1,0:T(8,128)} %get-tuple-element.296, f32[32,8,128,128]{2,3,1,0:T(8,128)} %get-tuple-element.294, f32[32,8,128,128]{2,3,1,0:T(8,128)} %get-tuple-element.295), kind=kLoop, calls=%fused_computation.320 | loop fusion | flops 16777216 | bytes 100663296 | tf_op jit(solution)/shard_map/add | solution.py:131
  667.8 17.4 %copy.108 = f32[32,8,128,128]{3,2,1,0:T(8,128)} copy(f32[32,8,128,128]{2,3,1,0:T(8,128)} %add_add_fusion) | data formatting | bytes 33554432 | tf_op jit(solution)/shard_map/add | solution.py:131
  685.4 0.9 copy-done.16
  687.1 1.0 copy.308
  688.9 1.2 bitcast_dynamic-update-slice_fusion.2
  690.3 1.0 copy.307
  691.2 1.2 bitcast_dynamic-update-slice_fusion
  692.4 368.8 %reduce-scatter.2.cloned.1.call-done = f32[4,128,128]{2,1,0:T(8,128)} async-done(((f32[256,128,128]{2,1,0:T(8,128)}), f32[4,128,128]{2,1,0:T(8,128)}) %reduce-scatter.2.cloned.1.call-update) | async-done | bytes 262160 | tf_op jit(solution)/shard_map/reduce_scatter | solution.py:133
  (118 shorter events, 9.5 us)
Async XLA Ops:
  7.2 117.7 %all-gather.3.cloned.1.call-start = ((), (), s32[]{:S(2)}) async-start(), calls=%async_computation.2 | async-start | bytes 8519680 | tf_op jit(solution)/shard_map/all_gather | solution.py:57
  7.9 1053.4 %reduce-scatter.2.cloned.1.call-start = ((), (), s32[]{:S(2)}) async-start(), calls=%async_computation.1 | async-start | bytes 17039360 | tf_op jit(solution)/shard_map/reduce_scatter | solution.py:133
  124.8 51.9 %copy-start.15 = (bf16[64,4096]{1,0:T(8,128)(2,1)}, bf16[64,4096]{1,0:T(8,128)(2,1)S(1)}, u32[]{:S(2)}) copy-start(bf16[64,4096]{1,0:T(8,128)(2,1)S(1)} %get-tuple-element.346) | copy-start | bytes 1572868
  124.8 50.6 %collective-permute-start = (bf16[64,4096]{1,0:T(8,128)(2,1)S(1)}, bf16[64,4096]{1,0:T(8,128)(2,1)S(1)}, u32[]{:S(2)}, u32[]{:S(2)}) collective-permute-start(bf16[64,4096]{1,0:T(8,128)(2,1)S(1)} %get-tuple-element.346), channel_id=1, source_target_pairs={{0,64},{64,128},{128,192},{1,65},{65,129},{129,193},{2,66},{66,130... | collective-permute-start | bytes 1572872 | tf_op jit(solution)/shard_map/ppermute | solution.py:16
  176.8 38.5 %copy-start.37 = (s32[2,1]{0,1:T(1,128)S(1)}, s32[2,1]{0,1:T(1,128)}, u32[]{:S(2)}) copy-start(s32[2,1]{0,1:T(1,128)} %param.33) | copy-start | bytes 28
  213.4 17.5 %copy-start.18 = (bf16[64,4096]{1,0:T(8,128)(2,1)}, bf16[64,4096]{1,0:T(8,128)(2,1)S(1)}, u32[]{:S(2)}) copy-start(bf16[64,4096]{1,0:T(8,128)(2,1)S(1)} %get-tuple-element.347) | copy-start | bytes 1572868
  213.4 16.2 %collective-permute-start.1 = (bf16[64,4096]{1,0:T(8,128)(2,1)S(1)}, bf16[64,4096]{1,0:T(8,128)(2,1)S(1)}, u32[]{:S(2)}, u32[]{:S(2)}) collective-permute-start(bf16[64,4096]{1,0:T(8,128)(2,1)S(1)} %get-tuple-element.347), channel_id=1, source_target_pairs={{0,64},{64,128},{128,192},{1,65},{65,129},{129,193},{2,66},{66,130... | collective-permute-start | bytes 1572872 | tf_op jit(solution)/shard_map/ppermute | solution.py:16
  267.5 16.6 %copy-start.20 = (bf16[64,4096]{1,0:T(8,128)(2,1)}, bf16[64,4096]{1,0:T(8,128)(2,1)S(1)}, u32[]{:S(2)}) copy-start(bf16[64,4096]{1,0:T(8,128)(2,1)S(1)} %get-tuple-element.348) | copy-start | bytes 1572868
  267.5 15.3 %collective-permute-start.2 = (bf16[64,4096]{1,0:T(8,128)(2,1)S(1)}, bf16[64,4096]{1,0:T(8,128)(2,1)S(1)}, u32[]{:S(2)}, u32[]{:S(2)}) collective-permute-start(bf16[64,4096]{1,0:T(8,128)(2,1)S(1)} %get-tuple-element.348), channel_id=1, source_target_pairs={{0,64},{64,128},{128,192},{1,65},{65,129},{129,193},{2,66},{66,130... | collective-permute-start | bytes 1572872 | tf_op jit(solution)/shard_map/ppermute | solution.py:16
  284.1 53.2 %copy-start.35 = (s32[1,256]{1,0:T(1,128)S(1)}, s32[1,256]{1,0:T(1,128)}, u32[]{:S(2)}) copy-start(s32[1,256]{1,0:T(1,128)} %param.32) | copy-start | bytes 3076
  284.3 53.0 %copy-start.22 = (bf16[64,4096]{1,0:T(8,128)(2,1)}, bf16[64,4096]{1,0:T(8,128)(2,1)S(1)}, u32[]{:S(2)}) copy-start(bf16[64,4096]{1,0:T(8,128)(2,1)S(1)} %get-tuple-element.349) | copy-start | bytes 1572868
  284.4 50.9 %collective-permute-start.3 = (bf16[64,4096]{1,0:T(8,128)(2,1)S(1)}, bf16[64,4096]{1,0:T(8,128)(2,1)S(1)}, u32[]{:S(2)}, u32[]{:S(2)}) collective-permute-start(bf16[64,4096]{1,0:T(8,128)(2,1)S(1)} %get-tuple-element.349), channel_id=1, source_target_pairs={{0,64},{64,128},{128,192},{1,65},{65,129},{129,193},{2,66},{66,130... | collective-permute-start | bytes 1572872 | tf_op jit(solution)/shard_map/ppermute | solution.py:16
  345.2 16.1 %collective-permute-start.4 = (bf16[64,4096]{1,0:T(8,128)(2,1)}, bf16[64,4096]{1,0:T(8,128)(2,1)S(1)}, u32[]{:S(2)}, u32[]{:S(2)}) collective-permute-start(bf16[64,4096]{1,0:T(8,128)(2,1)} %get-tuple-element.289), channel_id=1, source_target_pairs={{64,0},{128,64},{192,128},{65,1},{129,65},{193,129},{66,2},{130,66... | collective-permute-start | bytes 1572872 | tf_op jit(solution)/shard_map/ppermute | solution.py:16
  370.8 109.6 %copy-start.32 = (bf16[64,4096]{1,0:T(8,128)(2,1)}, bf16[64,4096]{1,0:T(8,128)(2,1)S(1)}, u32[]{:S(2)}) copy-start(bf16[64,4096]{1,0:T(8,128)(2,1)S(1)} %get-tuple-element.290) | copy-start | bytes 1572868
  370.8 107.6 %collective-permute-start.5 = (bf16[64,4096]{1,0:T(8,128)(2,1)S(1)}, bf16[64,4096]{1,0:T(8,128)(2,1)S(1)}, u32[]{:S(2)}, u32[]{:S(2)}) collective-permute-start(bf16[64,4096]{1,0:T(8,128)(2,1)S(1)} %get-tuple-element.290), channel_id=1, source_target_pairs={{64,0},{128,64},{192,128},{65,1},{129,65},{193,129},{66,2},{130,66... | collective-permute-start | bytes 1572872 | tf_op jit(solution)/shard_map/ppermute | solution.py:16
  481.2 9.1 copy-start.9
  516.5 4.5 copy-start.27
  518.0 3.1 copy-start.10
  521.1 10.2 copy-start.2
  538.9 14.4 %collective-permute-start.6 = (bf16[64,4096]{1,0:T(8,128)(2,1)}, bf16[64,4096]{1,0:T(8,128)(2,1)S(1)}, u32[]{:S(2)}, u32[]{:S(2)}) collective-permute-start(bf16[64,4096]{1,0:T(8,128)(2,1)} %get-tuple-element.291), channel_id=1, source_target_pairs={{64,0},{128,64},{192,128},{65,1},{129,65},{193,129},{66,2},{130,66... | collective-permute-start | bytes 1572872 | tf_op jit(solution)/shard_map/ppermute | solution.py:16
  554.5 69.1 %copy-start.36 = (f32[64]{0:T(128)S(1)}, f32[64]{0:T(128)}, u32[]{:S(2)}) copy-start(f32[64]{0:T(128)} %get-tuple-element.319) | copy-start | bytes 772
  555.4 9.1 copy-start.11
  590.7 3.5 copy-start.28
  591.2 3.1 copy-start.12
  594.2 8.4 copy-start.3
  610.3 13.3 %copy-start.33 = (bf16[64,4096]{1,0:T(8,128)(2,1)}, bf16[64,4096]{1,0:T(8,128)(2,1)S(1)}, u32[]{:S(2)}) copy-start(bf16[64,4096]{1,0:T(8,128)(2,1)S(1)} %get-tuple-element.292) | copy-start | bytes 1572868
  610.3 13.3 %collective-permute-start.7 = (bf16[64,4096]{1,0:T(8,128)(2,1)S(1)}, bf16[64,4096]{1,0:T(8,128)(2,1)S(1)}, u32[]{:S(2)}, u32[]{:S(2)}) collective-permute-start(bf16[64,4096]{1,0:T(8,128)(2,1)S(1)} %get-tuple-element.292), channel_id=1, source_target_pairs={{64,0},{128,64},{192,128},{65,1},{129,65},{193,129},{66,2},{130,66... | collective-permute-start | bytes 1572872 | tf_op jit(solution)/shard_map/ppermute | solution.py:16
  633.1 34.7 %copy-start.30 = (bf16[64,4096]{1,0:T(8,128)(2,1)}, bf16[64,4096]{1,0:T(8,128)(2,1)S(1)}, u32[]{:S(2)}) copy-start(bf16[64,4096]{1,0:T(8,128)(2,1)S(1)} %get-tuple-element.293) | copy-start | bytes 1572868
  685.2 1.0 copy-start.16
  685.2 1.4 copy-start.19
  685.2 1.5 copy-start.21
  685.3 2.8 copy-start.17
  685.3 2.8 copy-start.24
  685.3 1.7 copy-start.23
  688.4 2.8 copy-start.31
  688.4 1.7 copy-start.34
Sparse Core Ops, SparseCore 0:
  9.8 114.9 all-gather.2
  685.4 375.8 reduce-scatter.1
where the time goes:
time: 1080 us; the launch traced here: 1070 us
  waiting for transfers between devices  705 us (65%)
  other arithmetic  168 us (16%)
  matrix products  65.3 us (6%)
  starting transfers between devices  59.6 us (6%)
  local copies, waits for them, and re-layouts  53.2 us (5%)
  between operations  15.1 us (1%)
    reduce_scatter x1, waiting for transfers between devices, on_device(): lax.psum_scatter(tile_grads.reshape(blocks * KEEP, TILE, TILE), 'dp', sca...  369 us
    ppermute x8, waiting for transfers between devices, from_behind(): lax.ppermute(value, axis, [(source, source + steps) for source in range(l...  220 us
    all_gather x1, waiting for transfers between devices, on_device(): gathered = lax.all_gather(weights[0], 'dp', axis=0, tiled=True)  116 us
    scatter-add x4, other arithmetic, sparse_product(): placed.at[:, column_flat, :]  105 us
    ppermute x8, starting transfers between devices, from_behind(): lax.ppermute(value, axis, [(source, source + steps) for source in range(l...  59.5 us
    add x1, other arithmetic, on_device(): tile_grads = tile_grads + tile_term  34.7 us
    dot_general x4, matrix products, sparse_product(): jnp.einsum('trk,rjkn->trjn', hidden.reshape(row_count, blocks, TILE), til...  34.1 us
    another operation x10, local copies, waits for them, and re-layouts  24.3 us
  transfers between devices with their start and end apart: 10, of which 10 were waited for; matrix products, arithmetic and copies ran while one was open for 1% of the time, Pallas kernels for 0%

commit v1 on v0

v1 whole, which is shorter than its diff:
```python
import jax
import jax.numpy as jnp
from jax import lax
from jax.sharding import Mesh
from jax.sharding import PartitionSpec as P

TILE = 128
KEEP = 8
GROUP = ("dq", "zl", "core")


epsilon = 1e-05


def normalize(section_input, section_gain):
    values = section_input.astype(jnp.float32)
    inv_rms = lax.rsqrt(jnp.mean(values * values, axis=-1, keepdims=True) + epsilon)
    unit_rows = values * inv_rms
    return (values, inv_rms, unit_rows, (unit_rows * section_gain).astype(jnp.bfloat16))


def store_slot(buffer_all, new_value, micro_slot, is_live):
    old_value = lax.dynamic_index_in_dim(buffer_all, micro_slot, 0, keepdims=False)
    chosen = jnp.where(is_live, new_value, old_value)
    return lax.dynamic_update_index_in_dim(buffer_all, chosen, micro_slot, 0)


def reduce_tiles(tile_grads):
    core = lax.axis_index("core")
    chips = lax.axis_size("dq") * lax.axis_size("zl")
    pairs = tile_grads.reshape((chips, 2, -1) + tile_grads.shape[1:])
    send = lax.dynamic_index_in_dim(pairs, 1 - core, 1, keepdims=False)
    keep = lax.dynamic_index_in_dim(pairs, core, 1, keepdims=False)
    halved = keep + lax.ppermute(send, "core", [(0, 1), (1, 0)])
    spread = lax.all_to_all(halved, ("dq", "zl"), 0, 0, tiled=True)
    return spread.sum(axis=0)


def on_device(acts_in, cotangent, norm_gains, weights, tile_columns, lengths):
    micro_count, row_count, model_width = acts_in.shape
    section_count = lax.axis_size("pipe")
    section_here = lax.axis_index("pipe")
    blocks = model_width // TILE
    section_gain = norm_gains[0]
    column_list = tile_columns[0]
    column_table = column_list.reshape(blocks, KEEP)
    gathered = lax.all_gather(weights[0], GROUP, axis=0, tiled=True)
    tile_grid = gathered.reshape(blocks, KEEP, TILE, TILE)
    onehot = (column_table[:, :, None] == jnp.arange(blocks, dtype=jnp.int32)).astype(jnp.bfloat16)
    dense = (
        jnp.einsum("rjkn,rjc->rkcn", tile_grid, onehot, preferred_element_type=jnp.float32)
        .astype(jnp.bfloat16)
        .reshape(model_width, model_width)
    )
    within = jnp.arange(row_count, dtype=jnp.int32)
    valid_rows = (within[None, :] < lengths).astype(jnp.float32)
    received = jnp.zeros((row_count, model_width), jnp.bfloat16)
    section_out = jnp.zeros_like(acts_in)
    saved_inputs = jnp.zeros_like(acts_in)
    saved_hidden = jnp.zeros_like(acts_in)
    saved_pre = jnp.zeros(acts_in.shape, jnp.float32)

    def run_forward(section_input):
        values, inv_rms, unit_rows, hidden = normalize(section_input, section_gain)
        pre_act = jnp.dot(hidden, dense, preferred_element_type=jnp.float32)
        return ((values + jax.nn.silu(pre_act)).astype(jnp.bfloat16), pre_act, hidden)

    def skip_forward(section_input):
        return (
            section_input,
            jnp.zeros((row_count, model_width), jnp.float32),
            jnp.zeros((row_count, model_width), jnp.bfloat16),
        )

    for clock_tick in range(micro_count + section_count - 1):
        micro_index = clock_tick - section_here
        is_live = jnp.logical_and(micro_index >= 0, micro_index < micro_count)
        micro_slot = jnp.clip(micro_index, 0, micro_count - 1)
        first_input = lax.dynamic_index_in_dim(acts_in, micro_slot, 0, keepdims=False)
        section_input = jnp.where(section_here == 0, first_input, received)
        section_result, pre_act, hidden = lax.cond(
            is_live, run_forward, skip_forward, section_input
        )
        section_out = store_slot(section_out, section_result, micro_slot, is_live)
        saved_inputs = store_slot(saved_inputs, section_input, micro_slot, is_live)
        saved_hidden = store_slot(saved_hidden, hidden, micro_slot, is_live)
        saved_pre = store_slot(saved_pre, pre_act, micro_slot, is_live)
        pairs = [
            (source, source + 1)
            for source in range(section_count - 1)
            if 0 <= clock_tick - source < micro_count
        ]
        if pairs:
            received = lax.ppermute(section_result, "pipe", pairs)

    def run_backward(section_input, grad_input, pre_act):
        values, inv_rms, unit_rows, hidden = normalize(section_input, section_gain)
        sigmoid_part = jax.nn.sigmoid(pre_act)
        grad_float = grad_input.astype(jnp.float32)
        pre_delta = (grad_float * sigmoid_part * (1.0 + pre_act * (1.0 - sigmoid_part))).astype(
            jnp.bfloat16
        )
        hidden_delta = lax.dot_general(
            pre_delta, dense, (((1,), (1,)), ((), ())), preferred_element_type=jnp.float32
        )
        gained = hidden_delta * section_gain
        input_delta = grad_float + inv_rms * (
            gained - unit_rows * jnp.mean(gained * unit_rows, axis=-1, keepdims=True)
        )
        return (input_delta.astype(jnp.bfloat16), pre_delta)

    def skip_backward(section_input, grad_input, pre_act):
        return (grad_input, jnp.zeros_like(grad_input))

    received = jnp.zeros((row_count, model_width), jnp.bfloat16)
    input_grad = jnp.zeros_like(acts_in)
    saved_delta = jnp.zeros_like(acts_in)
    for clock_tick in range(micro_count + section_count - 1):
        micro_index = clock_tick - (section_count - 1 - section_here)
        is_live = jnp.logical_and(micro_index >= 0, micro_index < micro_count)
        micro_slot = jnp.clip(micro_index, 0, micro_count - 1)
        last_cot = lax.dynamic_index_in_dim(cotangent, micro_slot, 0, keepdims=False).astype(
            jnp.float32
        )
        last_mask = lax.dynamic_index_in_dim(valid_rows, micro_slot, 0, keepdims=False)
        last_grad = (last_cot * last_mask[:, None]).astype(jnp.bfloat16)
        grad_input = jnp.where(section_here == section_count - 1, last_grad, received)
        section_input = lax.dynamic_index_in_dim(saved_inputs, micro_slot, 0, keepdims=False)
        pre_act = lax.dynamic_index_in_dim(saved_pre, micro_slot, 0, keepdims=False)
        input_delta, pre_delta = lax.cond(
            is_live, run_backward, skip_backward, section_input, grad_input, pre_act
        )
        input_grad = store_slot(input_grad, input_delta, micro_slot, is_live)
        saved_delta = store_slot(saved_delta, pre_delta, micro_slot, is_live)
        pairs = [
            (source, source - 1)
            for source in range(1, section_count)
            if 0 <= clock_tick - (section_count - 1 - source) < micro_count
        ]
        if pairs:
            received = lax.ppermute(input_delta, "pipe", pairs)
    all_rows = micro_count * row_count
    picked = jnp.take(saved_delta.reshape(all_rows, blocks, TILE), column_table, axis=1)
    tile_grads = jnp.einsum(
        "trk,trjn->rjkn",
        saved_hidden.reshape(all_rows, blocks, TILE),
        picked,
        preferred_element_type=jnp.float32,
    )
    weight_grad = reduce_tiles(tile_grads.reshape(blocks * KEEP, TILE, TILE))
    return (section_out[None], input_grad[None], weight_grad[None])


def solution(mesh):
    dp_size = mesh.shape["dp"]
    split = Mesh(
        mesh.devices.reshape(mesh.shape["pipe"], dp_size // 4, 2, 2),
        ("pipe",) + GROUP,
    )
    placed = (
        P(None, GROUP, None),
        P(None, GROUP, None),
        P("pipe", None),
        P("pipe", GROUP, None, None),
        P("pipe", None),
        P(None, GROUP),
    )
    return jax.shard_map(
        on_device,
        mesh=split,
        in_specs=placed,
        out_specs=(
            P("pipe", None, GROUP, None),
            P("pipe", None, GROUP, None),
            P("pipe", GROUP, None, None),
        ),
        check_vma=False,
    )
```

time: 1080 us -> 727 us (0.67)
  the two profiles are of different devices: /device:TPU:64 before, /device:TPU:10 now
where the time goes in v1:
time: 727 us; the launch traced here: 717 us
  waiting for transfers between devices  420 us (58%)
  matrix products  95.3 us (13%)
  local copies, waits for them, and re-layouts  84.5 us (12%)
  other arithmetic  65.1 us (9%)
  starting transfers between devices  35.2 us (5%)
  between operations  15.4 us (2%)
    ppermute x4, waiting for transfers between devices, on_device(): received = lax.ppermute(input_delta, 'pipe', pairs)  146 us
    all_to_all x1, waiting for transfers between devices, reduce_tiles(): spread = lax.all_to_all(halved, ('dq', 'zl'), 0, 0, tiled=True)  142 us
    all_gather x1, waiting for transfers between devices, on_device(): gathered = lax.all_gather(weights[0], GROUP, axis=0, tiled=True)  106 us
    dot_general x2, matrix products, run_forward(): pre_act = jnp.dot(hidden, dense, preferred_element_type=jnp.float32)  35.7 us
    dot_general x2, matrix products, run_backward(): lax.dot_general(pre_delta, dense, (((1,), (1,)), ((), ())), preferred_ele...  31.5 us
    dynamic_update_slice x30, other arithmetic, store_slot(): return lax.dynamic_update_index_in_dim(buffer_all, chosen, micro_slot, 0)  31.1 us
    unnamed x71, local copies, waits for them, and re-layouts  28.6 us
    all_to_all x1, starting transfers between devices, reduce_tiles(): spread = lax.all_to_all(halved, ('dq', 'zl'), 0, 0, tiled=True)  22.5 us
  transfers between devices with their start and end apart: 11, of which 7 were waited for; matrix products, arithmetic and copies ran while one was open for 8% of the time, Pallas kernels for 0%

profile of v1, /device:TPU:10, one launch (start us, length us, event | category | flops | bytes accessed | tf_op | source)
XLA Modules:
  0.0 717.2 jit_solution(18169113809712951756)
XLA Ops:
  8.5 1.3 reduce.5
  13.4 2.0 select_dynamic-update-slice_fusion
  16.2 2.0 fusion.97
  18.2 106.4 %all-gather.3.cloned.1.call-done = bf16[1,256,128,128]{3,2,0,1:T(8,128)(2,1)} async-done(((bf16[1,4,128,128]{3,2,0,1:T(8,128)(2,1)}), bf16[1,256,128,128]{3,2,0,1:T(8,128)(2,1)}) %all-gather.3.cloned.1.call-update) | async-done | bytes 8388624 | tf_op jit(solution)/shard_map/all_gather | solution.py:47
  124.6 16.6 %convolution_convert_fusion = bf16[32,32,128,128]{3,1,2,0:T(8,128)(2,1)} fusion(bf16[32,8,128,128]{3,2,1,0:T(8,128)(2,1)} %bitcast.380, s32[32,8]{1,0:T(8,128)S(1)} %eq.13), kind=kOutput, calls=%fused_computation.152 | convolution fusion | flops 285220864 | bytes 41944064 | tf_op jit(solution)/shard_map/rjkn,rjc->rkcn/dot_general | solution.py:51
  141.2 22.7 %copy.36 = bf16[512,8,32,128]{3,1,2,0:T(8,128)(2,1)} copy(bf16[512,8,32,128]{3,2,1,0:T(8,128)(2,1)} %bitcast.372) | data formatting | bytes 67108864
  163.9 21.3 %conditional.10 = (bf16[64,4096]{1,0:T(8,128)(2,1)}, f32[64,4096]{1,0:T(8,128)}, bf16[64,4096]{1,0:T(8,128)(2,1)}) conditional(s32[]{:T(128)} %convert_element_type.245, bf16[64,4096]{1,0:T(8,128)(2,1)} %get-tuple-element.415, (bf16[64,4096]{1,0:T(8,128)(2,1)}, f32[1,4096]{1,0:T(1,128)S(1)}, bf16[4096,4096]{1,0:T(8,128)(2,1)}) %tuple.177), branch_computations={%region_0.1_spmd, %region_1.3_spmd} | conditional | flops 2151153664 | bytes 37766168 | solution.py:81
  163.9 1.2 fusion
  165.2 2.0 fusion.2
  167.2 18.0 %fusion.3 = (bf16[64,4096]{1,0:T(8,128)(2,1)}, f32[64,4096]{1,0:T(8,128)}) fusion(bf16[64,4096]{1,0:T(8,128)(2,1)} %get-tuple-element.275, bf16[64,4096]{1,0:T(8,128)(2,1)} %fusion.2, bf16[4096,4096]{1,0:T(8,128)(2,1)} %get-tuple-element.277), kind=kOutput, calls=%fused_computation.7 | convolution fusion | flops 2149318656 | bytes 36175872 | tf_op jit(solution)/shard_map/cond/branch_1_fun/dot_general | solution.py:65
  185.2 1.4 collective-permute-start
  186.8 1.3 bitcast_dynamic-update-slice_fusion.4
  189.4 1.2 constant_dynamic-slice_fusion.18
  190.6 8.2 %collective-permute-done = bf16[64,4096]{1,0:T(8,128)(2,1)S(1)} collective-permute-done((bf16[64,4096]{1,0:T(8,128)(2,1)}, bf16[64,4096]{1,0:T(8,128)(2,1)S(1)}, u32[]{:S(2)}, u32[]{:S(2)}) %collective-permute-start) | collective-permute-done | bytes 524320 | tf_op jit(solution)/shard_map/ppermute | solution.py:94
  199.8 19.1 %conditional.11 = (bf16[64,4096]{1,0:T(8,128)(2,1)S(1)}, f32[64,4096]{1,0:T(8,128)}, bf16[64,4096]{1,0:T(8,128)(2,1)}) conditional(s32[]{:T(128)} %convert_element_type.248, bf16[64,4096]{1,0:T(8,128)(2,1)S(1)} %get-tuple-element.383, (bf16[64,4096]{1,0:T(8,128)(2,1)S(1)}, f32[1,4096]{1,0:T(1,128)S(1)}, bf16[4096,4096]{1,0:T(8,128)(2,1)}) %tuple.178), branch_computations={%region_3.4_spmd, %region_4.6_spmd} | conditional | flops 2151153664 | bytes 37766168 | solution.py:81
  201.2 17.7 %fusion.7 = (bf16[64,4096]{1,0:T(8,128)(2,1)S(1)}, f32[64,4096]{1,0:T(8,128)}) fusion(bf16[64,4096]{1,0:T(8,128)(2,1)S(1)} %get-tuple-element.278, bf16[64,4096]{1,0:T(8,128)(2,1)} %fusion.6, bf16[4096,4096]{1,0:T(8,128)(2,1)} %get-tuple-element.280), kind=kOutput, calls=%fused_computation.15 | convolution fusion | flops 2149318656 | bytes 36175872 | tf_op jit(solution)/shard_map/cond/branch_1_fun/dot_general | solution.py:65
  219.0 5.4 collective-permute-start.1
  224.3 2.2 bitcast_dynamic-update-slice_fusion.8
  226.5 1.9 constant_dynamic-slice_fusion.2
  228.4 1.7 bitcast_dynamic-update-slice_fusion.3
  231.1 4.1 collective-permute-done.1
  235.5 1.9 conditional.12
  238.2 2.0 bitcast_dynamic-update-slice_fusion.7
  240.2 1.9 constant_dynamic-slice_fusion.1
  242.1 1.3 bitcast_dynamic-update-slice_fusion.2
  244.8 2.3 conditional.13
  248.0 2.0 bitcast_dynamic-update-slice_fusion.6
  250.0 1.9 constant_dynamic-slice_fusion
  251.9 1.3 bitcast_dynamic-update-slice_fusion.1
  255.5 1.6 bitcast_dynamic-update-slice_fusion
  258.8 2.0 bitcast_dynamic-update-slice_fusion.5
  261.0 2.8 copy.30
  264.6 1.3 fusion.98
  267.5 2.0 bitcast_dynamic-update-slice_fusion.13
  269.4 1.9 constant_dynamic-slice_fusion.6
  271.3 1.3 fusion.99
  273.7 1.3 collective-permute-start.6
  275.0 2.0 bitcast_dynamic-update-slice_fusion.12
  276.9 1.9 constant_dynamic-slice_fusion.5
  278.8 138.5 %collective-permute-done.6 = bf16[64,4096]{1,0:T(8,128)(2,1)S(1)} collective-permute-done((bf16[64,4096]{1,0:T(8,128)(2,1)S(1)}, bf16[64,4096]{1,0:T(8,128)(2,1)S(1)}, u32[]{:S(2)}, u32[]{:S(2)}) %collective-permute-start.6) | collective-permute-done | bytes 524320 | tf_op jit(solution)/shard_map/ppermute | solution.py:141
  417.3 1.3 fusion.100
  418.6 17.6 %conditional.18 = (bf16[64,4096]{1,0:T(8,128)(2,1)S(1)}, bf16[64,4096]{1,0:T(8,128)(2,1)}) conditional(s32[]{:T(128)} %convert_element_type.265, bf16[64,4096]{1,0:T(8,128)(2,1)S(1)} %fusion.100, (bf16[64,4096]{1,0:T(8,128)(2,1)S(1)}, bf16[2,64,4096]{2,1,0:T(8,128)(2,1)S(1)}, s32[]{:T(128)}, f32[2,64,4096]{2,1,0:T(8,128)S(1)}, ...), branch_computations={%region_27.28_spmd, %region_28.31_spmd} | conditional | flops 2154299392 | bytes 40913180 | solution.py:130
  418.6 1.4 fusion.65
  420.0 15.8 %fusion.61 = (f32[64]{0:T(128)S(1)}, f32[64,4096]{1,0:T(8,128)S(1)}) fusion(f32[64]{0:T(128)S(1)} %add_rsqrt_fusion.8, bf16[2,64,4096]{2,1,0:T(8,128)(2,1)S(1)} %get-tuple-element.309, s32[]{:T(128)} %get-tuple-element.310, f32[4096]{0:T(1024)S(1)} %bitcast.391, bf16[64,4096]{1,0:T(8,128)(2,1)} %get-tuple-element.467, ...), kind=kOutput, calls=%fused_computation.114 | convolution fusion | flops 2148794368 | bytes 35668484 | tf_op jit(solution)/shard_map/cond/branch_1_fun/dot_general | solution.py:103
  436.2 1.3 collective-permute-start.7
  437.5 2.1 bitcast_dynamic-update-slice_fusion.11
  439.6 1.9 constant_dynamic-slice_fusion.4
  441.5 7.4 %collective-permute-done.7 = bf16[64,4096]{1,0:T(8,128)(2,1)S(1)} collective-permute-done((bf16[64,4096]{1,0:T(8,128)(2,1)S(1)}, bf16[64,4096]{1,0:T(8,128)(2,1)S(1)}, u32[]{:S(2)}, u32[]{:S(2)}) %collective-permute-start.7) | collective-permute-done | bytes 524320 | tf_op jit(solution)/shard_map/ppermute | solution.py:141
  448.9 1.3 fusion.101
  450.2 17.8 %conditional.19 = (bf16[64,4096]{1,0:T(8,128)(2,1)S(1)}, bf16[64,4096]{1,0:T(8,128)(2,1)}) conditional(s32[]{:T(128)} %convert_element_type.269, bf16[64,4096]{1,0:T(8,128)(2,1)S(1)} %fusion.101, (bf16[64,4096]{1,0:T(8,128)(2,1)S(1)}, bf16[2,64,4096]{2,1,0:T(8,128)(2,1)S(1)}, s32[]{:T(128)}, f32[2,64,4096]{2,1,0:T(8,128)S(1)}, ...), branch_computations={%region_31.32_spmd, %region_32.35_spmd} | conditional | flops 2154299392 | bytes 40913180 | solution.py:130
  450.5 1.4 fusion.78
  451.9 15.8 %fusion.74 = (f32[64]{0:T(128)S(1)}, f32[64,4096]{1,0:T(8,128)S(1)}) fusion(f32[64]{0:T(128)S(1)} %add_rsqrt_fusion.9, bf16[2,64,4096]{2,1,0:T(8,128)(2,1)S(1)} %get-tuple-element.315, s32[]{:T(128)} %get-tuple-element.316, f32[4096]{0:T(1024)S(1)} %bitcast.392, bf16[64,4096]{1,0:T(8,128)(2,1)} %get-tuple-element.471, ...), kind=kOutput, calls=%fused_computation.136 | convolution fusion | flops 2148794368 | bytes 35668484 | tf_op jit(solution)/shard_map/cond/branch_1_fun/dot_general | solution.py:103
  468.0 2.3 bitcast_dynamic-update-slice_fusion.10
  470.3 1.5 copy.29
  472.2 8.7 %gather_fusion = bf16[256,128,128]{2,1,0:T(8,128)(2,1)} fusion(bf16[128,32,128]{2,0,1:T(8,128)(2,1)S(1)} %copy.20, s32[1024]{0:T(1024)S(1)} %copy-done.30), kind=kCustom, calls=%fused_computation | custom fusion | bytes 16778240 | tf_op jit(solution)/shard_map/jit(_take)/gather | solution.py:143
  480.9 12.0 %copy.21 = bf16[32,8,128,128]{2,3,1,0:T(8,128)(2,1)} copy(bf16[32,8,128,128]{3,2,1,0:T(8,128)(2,1)} %bitcast.375) | data formatting | bytes 16777216 | tf_op jit(solution)/shard_map/jit(_take)/gather | solution.py:143
  493.0 11.5 %fusion.85 = f32[32,8,128,128]{3,2,1,0:T(8,128)} fusion(bf16[32,8,128,128]{2,3,1,0:T(8,128)(2,1)} %copy.21, pred[32,8]{1,0:T(8,128)(4,1)S(1)} %copy-done.31, bf16[128,32,128,1]{2,1,0,3:T(8,128)(2,1)S(1)} %bitcast.381), kind=kOutput, calls=%fused_computation.154 | convolution fusion | flops 1077936128 | bytes 26214656 | tf_op jit(solution)/shard_map/trk,trjn->rjkn/dot_general | solution.py:144
  504.5 7.8 %dynamic-slice_bitcast_fusion = f32[32,4,128,128]{2,3,1,0:T(8,128)} fusion(f32[32,2,4,128,128]{3,4,2,1,0:T(8,128)} %bitcast.373, s32[]{:T(128)S(6)} %select_n.383), kind=kLoop, calls=%fused_computation.158 | loop fusion | bytes 16777220 | tf_op jit(solution)/shard_map/jit(dynamic_index_in_dim)/squeeze | solution.py:32
  512.5 13.5 %collective-permute-done.8 = f32[32,4,128,128]{2,3,1,0:T(8,128)} collective-permute-done((f32[32,4,128,128]{2,3,1,0:T(8,128)}, f32[32,4,128,128]{2,3,1,0:T(8,128)}, u32[]{:S(2)}, u32[]{:S(2)}) %collective-permute-start.8) | collective-permute-done | bytes 8388640 | tf_op jit(solution)/shard_map/ppermute | solution.py:34
  526.0 11.7 %bitcast_add_fusion = f32[32,4,128,128]{2,3,1,0:T(8,128)} fusion(f32[32,4,128,128]{2,3,1,0:T(8,128)} %collective-permute-done.8, f32[32,2,4,128,128]{3,4,2,1,0:T(8,128)} %bitcast.374, s32[]{:T(128)S(6)} %select_n.382), kind=kLoop, calls=%fused_computation.153 | loop fusion | flops 2097152 | bytes 25165828 | tf_op jit(solution)/shard_map/add | solution.py:34
  537.8 22.5 %all-to-all-start = ((f32[32,4,128,128]{2,3,1,0:T(8,128)}), f32[32,4,128,128]{2,3,1,0:T(8,128)}, u32[]{:S(2)}, u32[]{:S(2)}) async-start(f32[32,4,128,128]{2,3,1,0:T(8,128)} %bitcast_add_fusion), calls=%async_computation | async-start | bytes 16777216 | tf_op jit(solution)/shard_map/all_to_all | solution.py:35
  560.4 1.3 bitcast_dynamic-update-slice_fusion.28
  563.6 141.6 %all-to-all-done = f32[32,4,128,128]{2,3,1,0:T(8,128)} async-done(((f32[32,4,128,128]{2,3,1,0:T(8,128)}), f32[32,4,128,128]{2,3,1,0:T(8,128)}, u32[]{:S(2)}, u32[]{:S(2)}) %all-to-all-start) | async-done | bytes 8388640 | tf_op jit(solution)/shard_map/all_to_all | solution.py:35
  705.2 3.8 reduce_sum.164
  (146 shorter events, 32.6 us)
Async XLA Ops:
  7.2 117.5 %all-gather.3.cloned.1.call-start = ((), (), s32[]{:S(2)}) async-start(), calls=%async_computation.1 | async-start | bytes 8519680 | tf_op jit(solution)/shard_map/all_gather | solution.py:47
  141.2 22.7 %copy-start.27 = (f32[1,4096]{1,0:T(1,128)S(1)}, f32[1,4096]{1,0:T(1,128)}, u32[]{:S(2)}) copy-start(f32[1,4096]{1,0:T(1,128)} %param.28) | copy-start | bytes 49156
  185.2 13.6 %copy-start.21 = (bf16[2,64,4096]{2,1,0:T(8,128)(2,1)S(1)}, bf16[2,64,4096]{2,1,0:T(8,128)(2,1)}, u32[]{:S(2)}) copy-start(bf16[2,64,4096]{2,1,0:T(8,128)(2,1)} %param.26) | copy-start | bytes 3145732
  185.2 13.6 %copy-start.26 = (bf16[1,64,4096]{2,1,0:T(8,128)(2,1)S(1)}, bf16[1,64,4096]{2,1,0:T(8,128)(2,1)}, u32[]{:S(2)}) copy-start(bf16[1,64,4096]{2,1,0:T(8,128)(2,1)} %constant_dynamic-slice_fusion.22) | copy-start | bytes 1572868
  185.2 13.6 %collective-permute-start = (bf16[64,4096]{1,0:T(8,128)(2,1)}, bf16[64,4096]{1,0:T(8,128)(2,1)S(1)}, u32[]{:S(2)}, u32[]{:S(2)}) collective-permute-start(bf16[64,4096]{1,0:T(8,128)(2,1)} %get-tuple-element.348), channel_id=1, source_target_pairs={{0,64},{1,65},{2,66},{3,67},{4,68},{5,69},{6,70},{7,71},{8,72},{9,... | collective-permute-start | bytes 1572872 | tf_op jit(solution)/shard_map/ppermute | solution.py:94
  189.4 10.4 %copy-start = (bf16[2,64,4096]{2,1,0:T(8,128)(2,1)}, bf16[2,64,4096]{2,1,0:T(8,128)(2,1)S(1)}, u32[]{:S(2)}) copy-start(bf16[2,64,4096]{2,1,0:T(8,128)(2,1)S(1)} %bitcast_dynamic-update-slice_fusion.9) | copy-start | bytes 3145732
  219.0 16.5 %copy-start.2 = (bf16[64,4096]{1,0:T(8,128)(2,1)}, bf16[64,4096]{1,0:T(8,128)(2,1)S(1)}, u32[]{:S(2)}) copy-start(bf16[64,4096]{1,0:T(8,128)(2,1)S(1)} %get-tuple-element.349) | copy-start | bytes 1572868
  219.0 16.3 %copy-start.22 = (bf16[2,64,4096]{2,1,0:T(8,128)(2,1)S(1)}, bf16[2,64,4096]{2,1,0:T(8,128)(2,1)}, u32[]{:S(2)}) copy-start(bf16[2,64,4096]{2,1,0:T(8,128)(2,1)} %param.26) | copy-start | bytes 3145732
  219.0 16.3 %collective-permute-start.1 = (bf16[64,4096]{1,0:T(8,128)(2,1)S(1)}, bf16[64,4096]{1,0:T(8,128)(2,1)S(1)}, u32[]{:S(2)}, u32[]{:S(2)}) collective-permute-start(bf16[64,4096]{1,0:T(8,128)(2,1)S(1)} %get-tuple-element.349), channel_id=1, source_target_pairs={{0,64},{64,128},{1,65},{65,129},{2,66},{66,130},{3,67},{67,131},{4... | collective-permute-start | bytes 1572872 | tf_op jit(solution)/shard_map/ppermute | solution.py:94
  237.4 7.4 %copy-start.6 = (bf16[64,4096]{1,0:T(8,128)(2,1)}, bf16[64,4096]{1,0:T(8,128)(2,1)S(1)}, u32[]{:S(2)}) copy-start(bf16[64,4096]{1,0:T(8,128)(2,1)S(1)} %get-tuple-element.350) | copy-start | bytes 1572868
  237.4 7.2 copy-start.23
  237.4 7.1 collective-permute-start.2
  247.1 7.2 %copy-start.8 = (bf16[64,4096]{1,0:T(8,128)(2,1)}, bf16[64,4096]{1,0:T(8,128)(2,1)S(1)}, u32[]{:S(2)}) copy-start(bf16[64,4096]{1,0:T(8,128)(2,1)S(1)} %get-tuple-element.351) | copy-start | bytes 1572868
  247.1 7.2 copy-start.24
  247.1 7.2 collective-permute-start.3
  255.5 1.6 copy-start.4
  258.1 6.6 collective-permute-start.4
  261.0 5.0 copy-start.1
  266.8 5.8 copy-start.15
  266.8 4.5 collective-permute-start.5
  272.6 144.7 %copy-start.33 = (f32[64]{0:T(128)S(1)}, f32[64]{0:T(128)}, u32[]{:S(2)}) copy-start(f32[64]{0:T(128)} %get-tuple-element.417) | copy-start | bytes 772
  273.7 144.9 %copy-start.17 = (bf16[64,4096]{1,0:T(8,128)(2,1)}, bf16[64,4096]{1,0:T(8,128)(2,1)S(1)}, u32[]{:S(2)}) copy-start(bf16[64,4096]{1,0:T(8,128)(2,1)S(1)} %get-tuple-element.360) | copy-start | bytes 1572868
  273.7 143.6 %collective-permute-start.6 = (bf16[64,4096]{1,0:T(8,128)(2,1)S(1)}, bf16[64,4096]{1,0:T(8,128)(2,1)S(1)}, u32[]{:S(2)}, u32[]{:S(2)}) collective-permute-start(bf16[64,4096]{1,0:T(8,128)(2,1)S(1)} %get-tuple-element.360), channel_id=1, source_target_pairs={{64,0},{128,64},{65,1},{129,65},{66,2},{130,66},{67,3},{131,67},{6... | collective-permute-start | bytes 1572872 | tf_op jit(solution)/shard_map/ppermute | solution.py:141
  418.6 30.3 %copy-start.32 = (f32[64]{0:T(128)S(1)}, f32[64]{0:T(128)}, u32[]{:S(2)}) copy-start(f32[64]{0:T(128)} %get-tuple-element.416) | copy-start | bytes 772
  436.2 12.7 %copy-start.19 = (bf16[64,4096]{1,0:T(8,128)(2,1)}, bf16[64,4096]{1,0:T(8,128)(2,1)S(1)}, u32[]{:S(2)}) copy-start(bf16[64,4096]{1,0:T(8,128)(2,1)S(1)} %get-tuple-element.361) | copy-start | bytes 1572868
  436.2 12.7 %collective-permute-start.7 = (bf16[64,4096]{1,0:T(8,128)(2,1)S(1)}, bf16[64,4096]{1,0:T(8,128)(2,1)S(1)}, u32[]{:S(2)}, u32[]{:S(2)}) collective-permute-start(bf16[64,4096]{1,0:T(8,128)(2,1)S(1)} %get-tuple-element.361), channel_id=1, source_target_pairs={{64,0},{65,1},{66,2},{67,3},{68,4},{69,5},{70,6},{71,7},{72,8},{73... | collective-permute-start | bytes 1572872 | tf_op jit(solution)/shard_map/ppermute | solution.py:141
  450.2 22.1 %copy-start.30 = (s32[1024]{0:T(1024)S(1)}, s32[1024]{0:T(1024)}, u32[]{:S(2)}) copy-start(s32[1024]{0:T(1024)} %pad_clamp_fusion) | copy-start | bytes 12292
  468.0 3.8 copy-start.13
  480.9 12.1 %copy-start.25 = (bf16[16,8,32,128]{3,2,1,0:T(8,128)(2,1)S(1)}, bf16[16,8,32,128]{3,2,1,0:T(8,128)(2,1)}, u32[]{:S(2)}) copy-start(bf16[16,8,32,128]{3,2,1,0:T(8,128)(2,1)} %copy.30) | copy-start | bytes 3145732
  480.9 12.1 %copy-start.31 = (pred[32,8]{1,0:T(8,128)(4,1)S(1)}, pred[32,8]{1,0:T(8,128)(4,1)}, u32[]{:S(2)}) copy-start(pred[32,8]{1,0:T(8,128)(4,1)} %compare_and_fusion) | copy-start | bytes 772
  512.3 13.8 %collective-permute-start.8 = (f32[32,4,128,128]{2,3,1,0:T(8,128)}, f32[32,4,128,128]{2,3,1,0:T(8,128)}, u32[]{:S(2)}, u32[]{:S(2)}) collective-permute-start(f32[32,4,128,128]{2,3,1,0:T(8,128)} %dynamic-slice_bitcast_fusion), channel_id=1, source_target_pairs={{0,1},{1,0},{2,3},{3,2},{4,5},{5,4},{6,7},{7,6},{8,9},{9,8},{10,11... | collective-permute-start | bytes 25165832 | tf_op jit(solution)/shard_map/ppermute | solution.py:34
  537.8 23.9 %copy-start.3 = (bf16[64,4096]{1,0:T(8,128)(2,1)S(1)}, bf16[64,4096]{1,0:T(8,128)(2,1)}, u32[]{:S(2)}) copy-start(bf16[64,4096]{1,0:T(8,128)(2,1)} %copy-done.2) | copy-start | bytes 1572868
  537.8 24.1 %copy-start.7 = (bf16[64,4096]{1,0:T(8,128)(2,1)S(1)}, bf16[64,4096]{1,0:T(8,128)(2,1)}, u32[]{:S(2)}) copy-start(bf16[64,4096]{1,0:T(8,128)(2,1)} %copy-done.6) | copy-start | bytes 1572868
  537.8 167.4 %all-to-all-start = ((f32[32,4,128,128]{2,3,1,0:T(8,128)}), f32[32,4,128,128]{2,3,1,0:T(8,128)}, u32[]{:S(2)}, u32[]{:S(2)}) async-start(f32[32,4,128,128]{2,3,1,0:T(8,128)} %bitcast_add_fusion), calls=%async_computation | async-start | bytes 16777216 | tf_op jit(solution)/shard_map/all_to_all | solution.py:35
  560.2 1.9 copy-start.9
  560.2 2.2 copy-start.12
  560.3 2.4 copy-start.5
  560.3 2.5 copy-start.16
  561.7 1.3 copy-start.18
  561.9 1.3 copy-start.20
  562.1 1.3 copy-start.14
  562.8 146.2 %copy-start.28 = (bf16[1,2,64,4096]{3,2,1,0:T(8,128)(2,1)}, bf16[1,2,64,4096]{3,2,1,0:T(8,128)(2,1)S(1)}, u32[]{:S(2)}) copy-start(bf16[1,2,64,4096]{3,2,1,0:T(8,128)(2,1)S(1)} %bitcast_dynamic-update-slice_fusion.24) | copy-start | bytes 3145732
  563.6 146.3 %copy-start.29 = (bf16[1,2,64,4096]{3,2,1,0:T(8,128)(2,1)}, bf16[1,2,64,4096]{3,2,1,0:T(8,128)(2,1)S(1)}, u32[]{:S(2)}) copy-start(bf16[1,2,64,4096]{3,2,1,0:T(8,128)(2,1)S(1)} %bitcast_dynamic-update-slice_fusion.15) | copy-start | bytes 3145732
Sparse Core Ops, SparseCore 0:
  9.8 114.7 all-gather.2

commit v2 on v1

--- a/solution.py
+++ b/solution.py
@@ -36,7 +36,37 @@
     return spread.sum(axis=0)
 
 
+def gather_tiles(shard):
+    core = lax.axis_index("core")
+    chips = lax.axis_size("dq") * lax.axis_size("zl")
+    sent = jnp.broadcast_to(shard[None], (chips,) + shard.shape)
+    mine = lax.all_to_all(sent, ("dq", "zl"), 0, 0, tiled=True)
+    other = lax.ppermute(mine, "core", [(0, 1), (1, 0)])
+    both = jnp.where(core == 0, jnp.stack([mine, other], 1), jnp.stack([other, mine], 1))
+    return both.reshape((-1,) + shard.shape[1:])
+
+
 def on_device(acts_in, cotangent, norm_gains, weights, tile_columns, lengths):
+    micro_count, row_count, model_width = acts_in.shape
+    within = jnp.arange(row_count, dtype=jnp.int32)
+    valid_rows = (within[None, :] < lengths).astype(jnp.float32)
+    merged = (1, micro_count * row_count, model_width)
+    section_out, input_grad, weight_grad = run_pipeline(
+        acts_in.reshape(merged),
+        cotangent.reshape(merged),
+        norm_gains,
+        weights,
+        tile_columns,
+        valid_rows.reshape(merged[:2]),
+    )
+    return (
+        section_out.reshape(acts_in.shape)[None],
+        input_grad.reshape(acts_in.shape)[None],
+        weight_grad[None],
+    )
+
+
+def run_pipeline(acts_in, cotangent, norm_gains, weights, tile_columns, valid_rows):
     micro_count, row_count, model_width = acts_in.shape
     section_count = lax.axis_size("pipe")
     section_here = lax.axis_index("pipe")
@@ -44,7 +74,7 @@
     section_gain = norm_gains[0]
     column_list = tile_columns[0]
     column_table = column_list.reshape(blocks, KEEP)
-    gathered = lax.all_gather(weights[0], GROUP, axis=0, tiled=True)
+    gathered = gather_tiles(weights[0])
     tile_grid = gathered.reshape(blocks, KEEP, TILE, TILE)
     onehot = (column_table[:, :, None] == jnp.arange(blocks, dtype=jnp.int32)).astype(jnp.bfloat16)
     dense = (
@@ -52,8 +82,6 @@
         .astype(jnp.bfloat16)
         .reshape(model_width, model_width)
     )
-    within = jnp.arange(row_count, dtype=jnp.int32)
-    valid_rows = (within[None, :] < lengths).astype(jnp.float32)
     received = jnp.zeros((row_count, model_width), jnp.bfloat16)
     section_out = jnp.zeros_like(acts_in)
     saved_inputs = jnp.zeros_like(acts_in)
@@ -148,7 +176,7 @@
         preferred_element_type=jnp.float32,
     )
     weight_grad = reduce_tiles(tile_grads.reshape(blocks * KEEP, TILE, TILE))
-    return (section_out[None], input_grad[None], weight_grad[None])
+    return (section_out, input_grad, weight_grad)
 
 
 def solution(mesh):

time: 727 us -> 702 us (0.966)
  blocking collectives: 0 us -> 57.5 us
  matrix products: 95.3 us -> 58.6 us
  waiting for transfers between devices: 420 us -> 402 us
  between operations: 15.4 us -> 1.37 us
  local copies, waits for them, and re-layouts: 84.5 us -> 70.7 us
  starting transfers between devices: 35.2 us -> 44 us
  other arithmetic: 65.1 us -> 57.6 us
    all_gather x1 -> x0, waiting for transfers between devices: 106 us -> none  [on_device(): gathered = lax.all_gather(weights[0], GROUP, axis=0, tiled=True)]
    ppermute x8 -> x7, waiting for transfers between devices: 158 us -> 252 us  [the longest x3 224 us: run_pipeline(): received = lax.ppermute(input_delta, 'pipe', pairs)]
    all_to_all x0 -> x1, blocking collectives: none -> 57.5 us  [gather_tiles(): mine = lax.all_to_all(sent, ('dq', 'zl'), 0, 0, tiled=True)]
    dynamic_update_slice x30 -> x0, other arithmetic: 31.1 us -> none  [store_slot(): return lax.dynamic_update_index_in_dim(buffer_all, chosen, micro_slot, 0)]
    select_n x6 -> x14, other arithmetic: 7.1 us -> 33.2 us  [the longest x1 13.6 us: gather_tiles(): jnp.where(core == 0, jnp.stack([mine, other], 1), jnp.stack([other, mine]...]
    dot_general x2 -> x1, matrix products: 35.7 us -> 13.5 us  [run_forward(): pre_act = jnp.dot(hidden, dense, preferred_element_type=jnp.float32)]
    dynamic_slice x21 -> x0, local copies, waits for them, and re-layouts: 17.7 us -> none  [store_slot(): lax.dynamic_index_in_dim(buffer_all, micro_slot, 0, keepdims=False)]
    dot_general x2 -> x1, matrix products: 31.5 us -> 16.7 us  [run_backward(): lax.dot_general(pre_delta, dense, (((1,), (1,)), ((), ())), preferred_ele...]
  transfers between devices with their start and end apart: 11 -> 9, of which waited for: 7 -> 5; matrix products, arithmetic and copies ran while one was open for 8% -> 1% of each run, Pallas kernels for 0% -> 0%
where the time goes in v2:
time: 702 us; the launch traced here: 693 us
  waiting for transfers between devices  402 us (57%)
  local copies, waits for them, and re-layouts  70.7 us (10%)
  matrix products  58.6 us (8%)
  other arithmetic  57.6 us (8%)
  blocking collectives  57.5 us (8%)
  starting transfers between devices  44 us (6%)
    ppermute x3, waiting for transfers between devices, run_pipeline(): received = lax.ppermute(input_delta, 'pipe', pairs)  224 us
    all_to_all x1, waiting for transfers between devices, reduce_tiles(): spread = lax.all_to_all(halved, ('dq', 'zl'), 0, 0, tiled=True)  137 us
    all_to_all x1, blocking collectives, gather_tiles(): mine = lax.all_to_all(sent, ('dq', 'zl'), 0, 0, tiled=True)  57.5 us
    all_to_all x1, starting transfers between devices, reduce_tiles(): spread = lax.all_to_all(halved, ('dq', 'zl'), 0, 0, tiled=True)  34.6 us
    unnamed x32, local copies, waits for them, and re-layouts  26.8 us
    ppermute x3, waiting for transfers between devices, run_pipeline(): received = lax.ppermute(section_result, 'pipe', pairs)  21.8 us
    gather x2, local copies, waits for them, and re-layouts, run_pipeline(): jnp.take(saved_delta.reshape(all_rows, blocks, TILE), column_table, axis=1)  20.7 us
    dot_general x1, matrix products, run_pipeline(): jnp.einsum('rjkn,rjc->rkcn', tile_grid, onehot, preferred_element_type=jn...  16.9 us
  transfers between devices with their start and end apart: 9, of which 5 were waited for; matrix products, arithmetic and copies ran while one was open for 1% of the time, Pallas kernels for 0%

profile of v2, /device:TPU:10, one launch (start us, length us, event | category | flops | bytes accessed | tf_op | source)
XLA Modules:
  0.0 692.8 jit_solution(9496820022715145720)
XLA Ops:
  0.6 1.0 copy.78
  1.6 1.9 broadcast_in_dim.66
  3.6 57.5 %all_to_all.10 = bf16[32,4,128,128]{3,1,2,0:T(4,128)(2,1)} all-to-all(bf16[32,4,128,128]{3,1,2,0:T(4,128)(2,1)S(1)} %broadcast_in_dim.66), channel_id=1, replica_groups=mesh['pipe'=4,'dq'=16,'zl'=2,'core'=2] {'dq','zl'}, dimensions={0} | all-to-all | bytes 8388608 | tf_op jit(solution)/shard_map/all_to_all | solution.py:43
  61.1 0.5 broadcast.319
  61.6 0.7 reduce.5
  62.5 6.1 collective-permute-done
  68.6 13.6 %maximum_select_fusion = bf16[32,2,4,128,128]{4,2,1,3,0:T(4,128)(2,1)} fusion(bf16[32,1,4,128,128]{4,2,1,3,0:T(4,128)(2,1)} %bitcast.13, bf16[32,1,4,128,128]{4,2,1,3,0:T(4,128)(2,1)} %bitcast.12, pred[]{:T(512)S(6)} %eq.35), kind=kLoop, calls=%fused_computation.99 | loop fusion | flops 12582912 | bytes 16777216 | tf_op jit(solution)/shard_map/jit(_where)/select_n | solution.py:45
  82.1 16.9 %convolution_convert_fusion = bf16[32,32,128,128]{3,1,2,0:T(8,128)(2,1)} fusion(bf16[32,8,128,128]{3,1,2,0:T(8,128)(2,1)} %bitcast.94, s32[32,8]{1,0:T(8,128)S(1)} %eq.15), kind=kOutput, calls=%fused_computation.98 | convolution fusion | flops 285220864 | bytes 41944064 | tf_op jit(solution)/shard_map/rjkn,rjc->rkcn/dot_general | solution.py:81
  99.0 22.6 %copy.93 = bf16[512,8,32,128]{3,1,2,0:T(8,128)(2,1)} copy(bf16[512,8,32,128]{3,2,1,0:T(8,128)(2,1)} %bitcast.91) | data formatting | bytes 67108864
  121.7 15.1 %conditional.8 = (bf16[128,4096]{1,0:T(8,128)(2,1)S(1)}, f32[128,4096]{1,0:T(8,128)S(1)}, bf16[128,4096]{1,0:T(8,128)(2,1)}) conditional(s32[]{:T(128)} %convert_element_type.146, bf16[128,4096]{1,0:T(8,128)(2,1)S(1)} %bitcast_select_fusion.3, (bf16[128,4096]{1,0:T(8,128)(2,1)S(1)}, f32[1,4096]{1,0:T(1,128)S(1)}, bf16[4096,4096]{1,0:T(8,128)(2,1)}) %tuple.128), branch_computations={%region_0.1_spmd, %region_1.3_spmd} | conditional | flops 4302307328 | bytes 41961496 | solution.py:109
  122.0 1.3 fusion.2
  123.3 13.5 %fusion.3 = (bf16[128,4096]{1,0:T(8,128)(2,1)S(1)}, f32[128,4096]{1,0:T(8,128)S(1)}) fusion(bf16[128,4096]{1,0:T(8,128)(2,1)S(1)} %get-tuple-element.72, bf16[128,4096]{1,0:T(8,128)(2,1)} %fusion.2, bf16[4096,4096]{1,0:T(8,128)(2,1)} %get-tuple-element.74), kind=kOutput, calls=%fused_computation.7 | convolution fusion | flops 4298637312 | bytes 38797312 | tf_op jit(solution)/shard_map/cond/branch_1_fun/dot_general | solution.py:93
  136.8 1.3 copy-done.9
  138.1 2.4 collective-permute-start.1
  140.6 21.8 %collective-permute-done.1 = bf16[128,4096]{1,0:T(8,128)(2,1)} collective-permute-done((bf16[128,4096]{1,0:T(8,128)(2,1)S(1)}, bf16[128,4096]{1,0:T(8,128)(2,1)}, u32[]{:S(2)}, u32[]{:S(2)}) %collective-permute-start.1) | collective-permute-done | bytes 1048608 | tf_op jit(solution)/shard_map/ppermute | solution.py:122
  162.6 2.7 conditional.9
  162.7 1.5 broadcast.238
  164.2 1.1 broadcast.239
  165.3 0.7 collective-permute-start.2
  166.3 1.3 bitcast_select_fusion.1
  167.7 4.0 conditional.10
  167.7 1.0 copy.106
  168.7 1.6 broadcast.242
  170.3 1.1 broadcast.243
  171.7 1.7 collective-permute-start.3
  173.5 1.4 broadcast_select_fusion.3
  174.9 1.4 select_select_fusion.3
  176.4 1.3 conditional.11
  176.6 1.1 broadcast.247
  177.7 2.7 select_select_fusion
  180.4 1.3 conditional.12
  180.4 1.1 broadcast.250
  181.7 1.7 collective-permute-start.4
  183.4 3.0 broadcast_select_fusion.2
  186.3 1.1 conditional.13
  186.3 1.1 broadcast.254
  187.4 1.6 collective-permute-start.5
  189.1 3.0 broadcast_select_fusion.1
  192.0 1.2 conditional.14
  192.0 1.0 broadcast.258
  193.3 1.3 collective-permute-start.6
  194.8 1.4 select_bitcast_fusion
  196.2 1.2 copy.89
  197.4 223.8 %collective-permute-done.6 = bf16[128,4096]{1,0:T(8,128)(2,1)} collective-permute-done((bf16[128,4096]{1,0:T(8,128)(2,1)}, bf16[128,4096]{1,0:T(8,128)(2,1)}, u32[]{:S(2)}, u32[]{:S(2)}) %collective-permute-start.6) | collective-permute-done | bytes 1048608 | tf_op jit(solution)/shard_map/ppermute | solution.py:169
  421.3 2.6 broadcast_select_fusion
  423.9 22.2 %conditional.15 = (bf16[128,4096]{1,0:T(8,128)(2,1)}, bf16[128,4096]{1,0:T(8,128)(2,1)S(1)}) conditional(s32[]{:T(128)} %convert_element_type.149, bf16[128,4096]{1,0:T(8,128)(2,1)} %broadcast_select_fusion, (bf16[128,4096]{1,0:T(8,128)(2,1)}, bf16[128,4096]{1,0:T(8,128)(2,1)S(1)}, f32[128,4096]{1,0:T(8,128)S(1)}, bf16[4096,4096]{1,0:T(8,128)(2,1)}, ...), branch_computations={%region_24.25_spmd, %region_25.28_spmd} | conditional | flops 4308598784 | bytes 56644168 | solution.py:158
  423.9 2.2 fusion.49
  426.1 16.7 %fusion.45 = (f32[128]{0:T(128)S(1)}, f32[128,4096]{1,0:T(8,128)S(1)}) fusion(bf16[128,4096]{1,0:T(8,128)(2,1)S(1)} %get-tuple-element.100, f32[128]{0:T(128)S(1)} %add_rsqrt_fusion.7, f32[4096]{0:T(1024)S(1)} %bitcast.105, bf16[128,4096]{1,0:T(8,128)(2,1)S(1)} %get-tuple-element.250, bf16[4096,4096]{1,0:T(8,128)(2,1)} %get-tuple-element.102), kind=kOutput, calls=%fused_computation.88 | convolution fusion | flops 4297588736 | bytes 37766144 | tf_op jit(solution)/shard_map/cond/branch_1_fun/dot_general | solution.py:131
  442.9 3.0 fusion.50
  446.1 0.3 select_select_fusion.1
  446.4 0.7 copy.79
  447.1 0.7 copy.80
  447.8 8.6 %gather_fusion = bf16[256,128,128]{2,1,0:T(8,128)(2,1)} fusion(bf16[128,32,128]{2,0,1:T(8,128)(2,1)S(1)} %copy.80, s32[1024]{0:T(1024)S(1)} %pad_clamp_fusion), kind=kCustom, calls=%fused_computation | custom fusion | bytes 16778240 | tf_op jit(solution)/shard_map/jit(_take)/gather | solution.py:171
  456.4 12.1 %copy.81 = bf16[32,8,128,128]{2,3,1,0:T(8,128)(2,1)} copy(bf16[32,8,128,128]{3,2,1,0:T(8,128)(2,1)} %bitcast.95) | data formatting | bytes 16777216 | tf_op jit(solution)/shard_map/jit(_take)/gather | solution.py:171
  468.4 11.5 %fusion.52 = f32[32,8,128,128]{3,2,1,0:T(8,128)} fusion(bf16[32,8,128,128]{2,3,1,0:T(8,128)(2,1)} %copy.81, pred[32,8]{1,0:T(8,128)(4,1)S(1)} %compare_and_fusion, bf16[128,32,128,1]{2,1,0,3:T(8,128)(2,1)S(1)} %bitcast.96), kind=kOutput, calls=%fused_computation.101 | convolution fusion | flops 1077936128 | bytes 26214656 | tf_op jit(solution)/shard_map/trk,trjn->rjkn/dot_general | solution.py:172
  480.0 7.7 %dynamic-slice_bitcast_fusion = f32[32,4,128,128]{2,3,1,0:T(8,128)} fusion(f32[32,2,4,128,128]{3,4,2,1,0:T(8,128)} %bitcast.92, s32[]{:T(128)S(6)} %select_n.321), kind=kLoop, calls=%fused_computation.104 | loop fusion | bytes 16777220 | tf_op jit(solution)/shard_map/jit(dynamic_index_in_dim)/squeeze | solution.py:32
  487.7 13.5 %collective-permute-done.7 = f32[32,4,128,128]{2,3,1,0:T(8,128)} collective-permute-done((f32[32,4,128,128]{2,3,1,0:T(8,128)}, f32[32,4,128,128]{2,3,1,0:T(8,128)}, u32[]{:S(2)}, u32[]{:S(2)}) %collective-permute-start.7) | collective-permute-done | bytes 8388640 | tf_op jit(solution)/shard_map/ppermute | solution.py:34
  501.2 11.7 %bitcast_add_fusion = f32[32,4,128,128]{2,3,1,0:T(8,128)} fusion(f32[32,4,128,128]{2,3,1,0:T(8,128)} %collective-permute-done.7, f32[32,2,4,128,128]{3,4,2,1,0:T(8,128)} %bitcast.93, s32[]{:T(128)S(6)} %select_n.320), kind=kLoop, calls=%fused_computation.100 | loop fusion | flops 2097152 | bytes 25165828 | tf_op jit(solution)/shard_map/add | solution.py:34
  512.9 34.6 %all-to-all-start.1 = ((f32[32,4,128,128]{2,3,1,0:T(8,128)}), f32[32,4,128,128]{2,3,1,0:T(8,128)}, u32[]{:S(2)}, u32[]{:S(2)}) async-start(f32[32,4,128,128]{2,3,1,0:T(8,128)} %bitcast_add_fusion), calls=%async_computation.1 | async-start | bytes 16777216 | tf_op jit(solution)/shard_map/all_to_all | solution.py:35
  547.5 1.2 select_select_fusion.4
  548.7 2.4 select_select_fusion.2
  551.1 136.6 %all-to-all-done.1 = f32[32,4,128,128]{2,3,1,0:T(8,128)} async-done(((f32[32,4,128,128]{2,3,1,0:T(8,128)}), f32[32,4,128,128]{2,3,1,0:T(8,128)}, u32[]{:S(2)}, u32[]{:S(2)}) %all-to-all-start.1) | async-done | bytes 8388640 | tf_op jit(solution)/shard_map/all_to_all | solution.py:35
  687.7 3.8 reduce_sum.117
  691.5 0.8 copy.83
  (53 shorter events, 1.7 us)
Async XLA Ops:
  3.5 58.1 %copy-start.14 = (s32[1,256]{1,0:T(1,128)S(1)}, s32[1,256]{1,0:T(1,128)}, u32[]{:S(2)}) copy-start(s32[1,256]{1,0:T(1,128)} %param.26) | copy-start | bytes 3076
  3.5 58.8 %copy-start.4 = (bf16[2,64,4096]{2,1,0:T(8,128)(2,1)S(1)}, bf16[2,64,4096]{2,1,0:T(8,128)(2,1)}, u32[]{:S(2)}) copy-start(bf16[2,64,4096]{2,1,0:T(8,128)(2,1)} %param.22) | copy-start | bytes 3145732
  61.1 7.5 %collective-permute-start = (bf16[32,4,128,128]{3,1,2,0:T(4,128)(2,1)}, bf16[32,4,128,128]{3,1,2,0:T(4,128)(2,1)}, u32[]{:S(2)}, u32[]{:S(2)}) collective-permute-start(bf16[32,4,128,128]{3,1,2,0:T(4,128)(2,1)} %all_to_all.10), channel_id=1, source_target_pairs={{0,1},{1,0},{2,3},{3,2},{4,5},{5,4},{6,7},{7,6},{8,9},{9,8},{10,11... | collective-permute-start | bytes 12582920 | tf_op jit(solution)/shard_map/ppermute | solution.py:44
  99.0 22.6 %copy-start.13 = (f32[1,4096]{1,0:T(1,128)S(1)}, f32[1,4096]{1,0:T(1,128)}, u32[]{:S(2)}) copy-start(f32[1,4096]{1,0:T(1,128)} %param.24) | copy-start | bytes 49156
  136.8 1.3 copy-start.9
  138.1 24.5 %copy-start = (bf16[128,4096]{1,0:T(8,128)(2,1)}, bf16[128,4096]{1,0:T(8,128)(2,1)S(1)}, u32[]{:S(2)}) copy-start(bf16[128,4096]{1,0:T(8,128)(2,1)S(1)} %get-tuple-element.127) | copy-start | bytes 3145732
  138.1 24.3 %collective-permute-start.1 = (bf16[128,4096]{1,0:T(8,128)(2,1)S(1)}, bf16[128,4096]{1,0:T(8,128)(2,1)}, u32[]{:S(2)}, u32[]{:S(2)}) collective-permute-start(bf16[128,4096]{1,0:T(8,128)(2,1)S(1)} %get-tuple-element.127), channel_id=1, source_target_pairs={{0,64},{1,65},{2,66},{3,67},{4,68},{5,69},{6,70},{7,71},{8,72},{9,... | collective-permute-start | bytes 3145736 | tf_op jit(solution)/shard_map/ppermute | solution.py:122
  165.3 1.0 copy-start.11
  165.3 1.0 collective-permute-start.2
  167.7 5.7 copy-start.15
  167.7 5.8 copy-start.5
  171.7 3.2 collective-permute-start.3
  177.7 2.7 copy-start.2
  181.7 1.7 collective-permute-start.4
  187.4 1.6 collective-permute-start.5
  193.3 228.0 %collective-permute-start.6 = (bf16[128,4096]{1,0:T(8,128)(2,1)}, bf16[128,4096]{1,0:T(8,128)(2,1)}, u32[]{:S(2)}, u32[]{:S(2)}) collective-permute-start(bf16[128,4096]{1,0:T(8,128)(2,1)} %get-tuple-element.137), channel_id=1, source_target_pairs={{64,0},{65,1},{66,2},{67,3},{68,4},{69,5},{70,6},{71,7},{72,8},{73... | collective-permute-start | bytes 3145736 | tf_op jit(solution)/shard_map/ppermute | solution.py:169
  196.2 225.0 %copy-start.6 = (bf16[2,64,4096]{2,1,0:T(8,128)(2,1)S(1)}, bf16[2,64,4096]{2,1,0:T(8,128)(2,1)}, u32[]{:S(2)}) copy-start(bf16[2,64,4096]{2,1,0:T(8,128)(2,1)} %param.23) | copy-start | bytes 3145732
  426.1 16.8 %copy-start.7 = (bf16[128,4096]{1,0:T(8,128)(2,1)}, bf16[128,4096]{1,0:T(8,128)(2,1)S(1)}, u32[]{:S(2)}) copy-start(bf16[128,4096]{1,0:T(8,128)(2,1)S(1)} %get-tuple-element.250) | copy-start | bytes 3145732 | tf_op jit(solution)/shard_map/cond
  442.9 3.0 copy-start.8
  456.4 12.1 %copy-start.10 = (bf16[16,8,32,128]{3,2,1,0:T(8,128)(2,1)S(1)}, bf16[16,8,32,128]{3,2,1,0:T(8,128)(2,1)}, u32[]{:S(2)}) copy-start(bf16[16,8,32,128]{3,2,1,0:T(8,128)(2,1)} %copy.89) | copy-start | bytes 3145732
  487.7 13.5 %collective-permute-start.7 = (f32[32,4,128,128]{2,3,1,0:T(8,128)}, f32[32,4,128,128]{2,3,1,0:T(8,128)}, u32[]{:S(2)}, u32[]{:S(2)}) collective-permute-start(f32[32,4,128,128]{2,3,1,0:T(8,128)} %dynamic-slice_bitcast_fusion), channel_id=1, source_target_pairs={{0,1},{1,0},{2,3},{3,2},{4,5},{5,4},{6,7},{7,6},{8,9},{9,8},{10,11... | collective-permute-start | bytes 25165832 | tf_op jit(solution)/shard_map/ppermute | solution.py:34
  512.9 34.6 %copy-start.1 = (bf16[128,4096]{1,0:T(8,128)(2,1)S(1)}, bf16[128,4096]{1,0:T(8,128)(2,1)}, u32[]{:S(2)}) copy-start(bf16[128,4096]{1,0:T(8,128)(2,1)} %copy-done) | copy-start | bytes 3145732
  512.9 34.6 %copy-start.3 = (bf16[128,4096]{1,0:T(8,128)(2,1)S(1)}, bf16[128,4096]{1,0:T(8,128)(2,1)}, u32[]{:S(2)}) copy-start(bf16[128,4096]{1,0:T(8,128)(2,1)} %copy-done.2) | copy-start | bytes 3145732
  512.9 34.6 %copy-start.12 = (bf16[128,4096]{1,0:T(8,128)(2,1)S(1)}, bf16[128,4096]{1,0:T(8,128)(2,1)}, u32[]{:S(2)}) copy-start(bf16[128,4096]{1,0:T(8,128)(2,1)} %copy-done.11) | copy-start | bytes 3145732
  512.9 174.8 %all-to-all-start.1 = ((f32[32,4,128,128]{2,3,1,0:T(8,128)}), f32[32,4,128,128]{2,3,1,0:T(8,128)}, u32[]{:S(2)}, u32[]{:S(2)}) async-start(f32[32,4,128,128]{2,3,1,0:T(8,128)} %bitcast_add_fusion), calls=%async_computation.1 | async-start | bytes 16777216 | tf_op jit(solution)/shard_map/all_to_all | solution.py:35

commit v3 on v2

--- a/solution.py
+++ b/solution.py
@@ -25,25 +25,27 @@
     return lax.dynamic_update_index_in_dim(buffer_all, chosen, micro_slot, 0)
 
 
-def reduce_tiles(tile_grads):
+def reduce_tiles(hidden_rows, delta_rows, column_table):
     core = lax.axis_index("core")
-    chips = lax.axis_size("dq") * lax.axis_size("zl")
-    pairs = tile_grads.reshape((chips, 2, -1) + tile_grads.shape[1:])
-    send = lax.dynamic_index_in_dim(pairs, 1 - core, 1, keepdims=False)
-    keep = lax.dynamic_index_in_dim(pairs, core, 1, keepdims=False)
-    halved = keep + lax.ppermute(send, "core", [(0, 1), (1, 0)])
-    spread = lax.all_to_all(halved, ("dq", "zl"), 0, 0, tiled=True)
+    half = column_table.shape[1] // 2
+
+    def tile_sums(columns):
+        picked = jnp.take(delta_rows, columns, axis=1)
+        return jnp.einsum("trk,trjn->rjkn", hidden_rows, picked, preferred_element_type=jnp.float32)
+
+    send = tile_sums(lax.dynamic_slice_in_dim(column_table, (1 - core) * half, half, 1))
+    got = lax.ppermute(send, "core", [(0, 1), (1, 0)])
+    keep = tile_sums(lax.dynamic_slice_in_dim(column_table, core * half, half, 1))
+    spread = lax.all_to_all(keep + got, ("dq", "zl"), 0, 0, tiled=True)
     return spread.sum(axis=0)
 
 
 def gather_tiles(shard):
-    core = lax.axis_index("core")
     chips = lax.axis_size("dq") * lax.axis_size("zl")
     sent = jnp.broadcast_to(shard[None], (chips,) + shard.shape)
     mine = lax.all_to_all(sent, ("dq", "zl"), 0, 0, tiled=True)
     other = lax.ppermute(mine, "core", [(0, 1), (1, 0)])
-    both = jnp.where(core == 0, jnp.stack([mine, other], 1), jnp.stack([other, mine], 1))
-    return both.reshape((-1,) + shard.shape[1:])
+    return jnp.stack([mine, other], 1).reshape((-1,) + shard.shape[1:])
 
 
 def on_device(acts_in, cotangent, norm_gains, weights, tile_columns, lengths):
@@ -76,7 +78,10 @@
     column_table = column_list.reshape(blocks, KEEP)
     gathered = gather_tiles(weights[0])
     tile_grid = gathered.reshape(blocks, KEEP, TILE, TILE)
-    onehot = (column_table[:, :, None] == jnp.arange(blocks, dtype=jnp.int32)).astype(jnp.bfloat16)
+    core = lax.axis_index("core")
+    local_order = (jnp.arange(KEEP, dtype=jnp.int32) + (KEEP // 2) * core) % KEEP
+    local_table = jnp.take(column_table, local_order, axis=1)
+    onehot = (local_table[:, :, None] == jnp.arange(blocks, dtype=jnp.int32)).astype(jnp.bfloat16)
     dense = (
         jnp.einsum("rjkn,rjc->rkcn", tile_grid, onehot, preferred_element_type=jnp.float32)
         .astype(jnp.bfloat16)
@@ -168,14 +173,11 @@
         if pairs:
             received = lax.ppermute(input_delta, "pipe", pairs)
     all_rows = micro_count * row_count
-    picked = jnp.take(saved_delta.reshape(all_rows, blocks, TILE), column_table, axis=1)
-    tile_grads = jnp.einsum(
-        "trk,trjn->rjkn",
+    weight_grad = reduce_tiles(
         saved_hidden.reshape(all_rows, blocks, TILE),
-        picked,
-        preferred_element_type=jnp.float32,
-    )
-    weight_grad = reduce_tiles(tile_grads.reshape(blocks * KEEP, TILE, TILE))
+        saved_delta.reshape(all_rows, blocks, TILE),
+        column_table,
+    )
     return (section_out, input_grad, weight_grad)
 
 

time: 702 us -> 673 us (0.959)
  other arithmetic: 57.6 us -> 41.1 us
  local copies, waits for them, and re-layouts: 70.7 us -> 62.1 us
    select_n x2, other arithmetic: 13.6 us -> 0.09 us  [run_pipeline(): local_table = jnp.take(column_table, local_order, axis=1)]
    add x1 -> x0, other arithmetic: 11.7 us -> none  [reduce_tiles(): halved = keep + lax.ppermute(send, 'core', [(0, 1), (1, 0)])]
    ppermute x1, waiting for transfers between devices: 13.5 us -> 3.87 us  [reduce_tiles(): got = lax.ppermute(send, 'core', [(0, 1), (1, 0)])]
    another operation x0 -> x1, other arithmetic: none -> 8.54 us  [gather_tiles(): return jnp.stack([mine, other], 1).reshape((-1,) + shard.shape[1:])]
    squeeze x1 -> x0, local copies, waits for them, and re-layouts: 7.72 us -> none  [reduce_tiles(): send = lax.dynamic_index_in_dim(pairs, 1 - core, 1, keepdims=False)]
    dot_general x1 -> x2, matrix products: 11.5 us -> 15.9 us  [tile_sums(): jnp.einsum('trk,trjn->rjkn', hidden_rows, picked, preferred_element_type=...]
    gather x2 -> x5, local copies, waits for them, and re-layouts: 20.7 us -> 19.6 us  [the longest x4 19.1 us: tile_sums(): picked = jnp.take(delta_rows, columns, axis=1)]
  transfers between devices with their start and end apart: 9 -> 9, of which waited for: 5 -> 5; matrix products, arithmetic and copies ran while one was open for 1% -> 3% of each run, Pallas kernels for 0% -> 0%
where the time goes in v3:
time: 673 us; the launch traced here: 665 us
  waiting for transfers between devices  396 us (59%)
  matrix products  63 us (9%)
  local copies, waits for them, and re-layouts  62.1 us (9%)
  blocking collectives  57.5 us (9%)
  starting transfers between devices  42.7 us (6%)
  other arithmetic  41.1 us (6%)
    ppermute x3, waiting for transfers between devices, run_pipeline(): received = lax.ppermute(input_delta, 'pipe', pairs)  225 us
    all_to_all x1, waiting for transfers between devices, reduce_tiles(): spread = lax.all_to_all(keep + got, ('dq', 'zl'), 0, 0, tiled=True)  140 us
    all_to_all x1, blocking collectives, gather_tiles(): mine = lax.all_to_all(sent, ('dq', 'zl'), 0, 0, tiled=True)  57.5 us
    all_to_all x1, starting transfers between devices, reduce_tiles(): spread = lax.all_to_all(keep + got, ('dq', 'zl'), 0, 0, tiled=True)  33.4 us
    unnamed x32, local copies, waits for them, and re-layouts  26.8 us
    ppermute x3, waiting for transfers between devices, run_pipeline(): received = lax.ppermute(section_result, 'pipe', pairs)  22.1 us
    gather x4, local copies, waits for them, and re-layouts, tile_sums(): picked = jnp.take(delta_rows, columns, axis=1)  19.1 us
    dot_general x1, matrix products, run_pipeline(): jnp.einsum('rjkn,rjc->rkcn', tile_grid, onehot, preferred_element_type=jn...  16.9 us
  transfers between devices with their start and end apart: 9, of which 5 were waited for; matrix products, arithmetic and copies ran while one was open for 3% of the time, Pallas kernels for 0%

profile of v3, /device:TPU:10, one launch (start us, length us, event | category | flops | bytes accessed | tf_op | source)
XLA Modules:
  0.0 664.6 jit_solution(11753234250350834097)
XLA Ops:
  0.6 1.0 copy.105
  1.6 1.9 broadcast_in_dim.78
  3.6 57.5 %all_to_all.10 = bf16[32,4,128,128]{3,1,2,0:T(4,128)(2,1)} all-to-all(bf16[32,4,128,128]{3,1,2,0:T(4,128)(2,1)S(1)} %broadcast_in_dim.78), channel_id=1, replica_groups=mesh['pipe'=4,'dq'=16,'zl'=2,'core'=2] {'dq','zl'}, dimensions={0} | all-to-all | bytes 8388608 | tf_op jit(solution)/shard_map/all_to_all | solution.py:46
  61.6 0.7 reduce.3
  62.5 0.6 gather_fusion
  63.3 5.3 collective-permute-done
  68.6 8.5 %pad_maximum_fusion = bf16[32,2,4,128,128]{4,2,1,3,0:T(4,128)(2,1)} fusion(bf16[32,1,4,128,128]{4,2,1,3,0:T(4,128)(2,1)} %bitcast.16, bf16[32,1,4,128,128]{4,2,1,3,0:T(4,128)(2,1)} %bitcast.15), kind=kLoop, calls=%fused_computation.101 | loop fusion | flops 4194304 | bytes 16777216 | tf_op jit(solution)/shard_map/stack | solution.py:48
  77.1 16.9 %convolution_convert_fusion = bf16[32,32,128,128]{3,1,2,0:T(8,128)(2,1)} fusion(bf16[32,8,128,128]{3,1,2,0:T(8,128)(2,1)} %bitcast.101, s32[32,8]{1,0:T(8,128)S(1)} %copy.104), kind=kOutput, calls=%fused_computation.100 | convolution fusion | flops 285220864 | bytes 41944064 | tf_op jit(solution)/shard_map/rjkn,rjc->rkcn/dot_general | solution.py:86
  94.0 22.6 %copy.129 = bf16[512,8,32,128]{3,1,2,0:T(8,128)(2,1)} copy(bf16[512,8,32,128]{3,2,1,0:T(8,128)(2,1)} %bitcast.100) | data formatting | bytes 67108864
  116.6 15.1 %conditional.8 = (bf16[128,4096]{1,0:T(8,128)(2,1)S(1)}, f32[128,4096]{1,0:T(8,128)S(1)}, bf16[128,4096]{1,0:T(8,128)(2,1)}) conditional(s32[]{:T(128)} %convert_element_type.146, bf16[128,4096]{1,0:T(8,128)(2,1)S(1)} %bitcast_select_fusion.3, (bf16[128,4096]{1,0:T(8,128)(2,1)S(1)}, f32[1,4096]{1,0:T(1,128)S(1)}, bf16[4096,4096]{1,0:T(8,128)(2,1)}) %tuple.133), branch_computations={%region_0.1_spmd, %region_1.3_spmd} | conditional | flops 4302307328 | bytes 41961496 | solution.py:114
  117.0 1.3 fusion.2
  118.3 13.5 %fusion.3 = (bf16[128,4096]{1,0:T(8,128)(2,1)S(1)}, f32[128,4096]{1,0:T(8,128)S(1)}) fusion(bf16[128,4096]{1,0:T(8,128)(2,1)S(1)} %get-tuple-element.73, bf16[128,4096]{1,0:T(8,128)(2,1)} %fusion.2, bf16[4096,4096]{1,0:T(8,128)(2,1)} %get-tuple-element.75), kind=kOutput, calls=%fused_computation.9 | convolution fusion | flops 4298637312 | bytes 38797312 | tf_op jit(solution)/shard_map/cond/branch_1_fun/dot_general | solution.py:98
  131.8 1.3 copy-done.10
  133.1 2.3 collective-permute-start.1
  135.3 22.1 %collective-permute-done.1 = bf16[128,4096]{1,0:T(8,128)(2,1)} collective-permute-done((bf16[128,4096]{1,0:T(8,128)(2,1)S(1)}, bf16[128,4096]{1,0:T(8,128)(2,1)}, u32[]{:S(2)}, u32[]{:S(2)}) %collective-permute-start.1) | collective-permute-done | bytes 1048608 | tf_op jit(solution)/shard_map/ppermute | solution.py:127
  157.6 3.2 conditional.9
  157.7 1.5 broadcast.316
  159.2 1.1 broadcast.317
  160.8 0.7 collective-permute-start.2
  161.8 1.3 bitcast_select_fusion.1
  163.1 3.6 conditional.10
  163.1 1.0 copy.142
  164.1 1.6 broadcast.320
  165.7 1.1 broadcast.321
  166.8 1.8 collective-permute-start.3
  168.7 1.4 broadcast_select_fusion.3
  170.1 1.4 select_select_fusion.3
  171.6 1.3 conditional.11
  171.8 1.1 broadcast.325
  172.9 2.7 select_select_fusion
  175.6 1.1 conditional.12
  175.6 1.1 broadcast.328
  176.7 1.7 collective-permute-start.4
  178.4 3.0 broadcast_select_fusion.2
  181.4 1.3 conditional.13
  181.4 1.1 broadcast.332
  182.6 1.6 collective-permute-start.5
  184.3 3.0 broadcast_select_fusion.1
  187.2 1.1 conditional.14
  187.2 1.1 broadcast.336
  188.3 1.3 collective-permute-start.6
  189.8 1.4 select_bitcast_fusion
  191.3 1.2 copy.123
  192.5 224.9 %collective-permute-done.6 = bf16[128,4096]{1,0:T(8,128)(2,1)} collective-permute-done((bf16[128,4096]{1,0:T(8,128)(2,1)}, bf16[128,4096]{1,0:T(8,128)(2,1)}, u32[]{:S(2)}, u32[]{:S(2)}) %collective-permute-start.6) | collective-permute-done | bytes 1048608 | tf_op jit(solution)/shard_map/ppermute | solution.py:174
  417.4 2.6 broadcast_select_fusion
  420.0 22.2 %conditional.15 = (bf16[128,4096]{1,0:T(8,128)(2,1)}, bf16[128,4096]{1,0:T(8,128)(2,1)S(1)}) conditional(s32[]{:T(128)} %convert_element_type.149, bf16[128,4096]{1,0:T(8,128)(2,1)} %broadcast_select_fusion, (bf16[128,4096]{1,0:T(8,128)(2,1)}, bf16[128,4096]{1,0:T(8,128)(2,1)S(1)}, f32[128,4096]{1,0:T(8,128)S(1)}, bf16[4096,4096]{1,0:T(8,128)(2,1)}, ...), branch_computations={%region_24.25_spmd, %region_25.28_spmd} | conditional | flops 4308598784 | bytes 56644168 | solution.py:163
  420.2 2.2 fusion.49
  422.4 16.8 %fusion.45 = (f32[128]{0:T(128)S(1)}, f32[128,4096]{1,0:T(8,128)S(1)}) fusion(bf16[128,4096]{1,0:T(8,128)(2,1)S(1)} %get-tuple-element.101, f32[128]{0:T(128)S(1)} %add_rsqrt_fusion.7, f32[4096]{0:T(1024)S(1)} %bitcast.114, bf16[128,4096]{1,0:T(8,128)(2,1)S(1)} %get-tuple-element.257, bf16[4096,4096]{1,0:T(8,128)(2,1)} %get-tuple-element.103), kind=kOutput, calls=%fused_computation.90 | convolution fusion | flops 4297588736 | bytes 37766144 | tf_op jit(solution)/shard_map/cond/branch_1_fun/dot_general | solution.py:136
  439.2 3.0 fusion.50
  442.5 0.7 copy.107
  443.2 0.7 copy.108
  443.9 3.0 gather_fusion.2
  446.9 6.5 copy.112
  453.4 6.7 %fusion.62 = f32[32,4,128,128]{2,3,1,0:T(8,128)} fusion(bf16[32,4,128,128]{2,3,1,0:T(8,128)(2,1)} %copy.112, pred[32,4]{1,0:T(8,128)(4,1)S(1)} %get-tuple-element.216, bf16[128,32,128,1]{2,1,0,3:T(8,128)(2,1)S(1)} %bitcast.104), kind=kOutput, calls=%fused_computation.111 | convolution fusion | flops 538968064 | bytes 13631616 | tf_op jit(solution)/shard_map/trk,trjn->rjkn/dot_general | solution.py:34
  460.3 3.1 gather_fusion.1
  463.3 6.5 copy.109
  469.8 3.9 collective-permute-done.7
  473.6 9.2 %bitcast_add_fusion = f32[32,4,128,128]{2,3,1,0:T(8,128)} fusion(f32[32,4,128,128]{2,3,1,0:T(8,128)} %collective-permute-done.7, bf16[32,4,128,128]{2,3,1,0:T(8,128)(2,1)} %copy.109, pred[32,4]{1,0:T(8,128)(4,1)S(1)} %get-tuple-element.186, bf16[128,32,128,1]{2,1,0,3:T(8,128)(2,1)S(1)} %bitcast.105), kind=kOutput, calls=%fused_computation.102 | convolution fusion | flops 541065216 | bytes 22020224 | tf_op jit(solution)/shard_map/trk,trjn->rjkn/dot_general | solution.py:34
  482.9 33.4 %all-to-all-start.1 = ((f32[32,4,128,128]{2,3,1,0:T(8,128)}), f32[32,4,128,128]{2,3,1,0:T(8,128)}, u32[]{:S(2)}, u32[]{:S(2)}) async-start(f32[32,4,128,128]{2,3,1,0:T(8,128)} %bitcast_add_fusion), calls=%async_computation.1 | async-start | bytes 16777216 | tf_op jit(solution)/shard_map/all_to_all | solution.py:39
  516.3 1.2 select_select_fusion.4
  517.4 2.4 select_select_fusion.2
  519.8 139.6 %all-to-all-done.1 = f32[32,4,128,128]{2,3,1,0:T(8,128)} async-done(((f32[32,4,128,128]{2,3,1,0:T(8,128)}), f32[32,4,128,128]{2,3,1,0:T(8,128)}, u32[]{:S(2)}, u32[]{:S(2)}) %all-to-all-start.1) | async-done | bytes 8388640 | tf_op jit(solution)/shard_map/all_to_all | solution.py:39
  659.5 3.8 reduce_sum.117
  663.3 0.8 copy.114
  (61 shorter events, 2.9 us)
Async XLA Ops:
  3.5 58.1 %copy-start.14 = (s32[1,256]{1,0:T(1,128)S(1)}, s32[1,256]{1,0:T(1,128)}, u32[]{:S(2)}) copy-start(s32[1,256]{1,0:T(1,128)} %param.28) | copy-start | bytes 3076
  3.5 59.7 %copy-start.4 = (bf16[2,64,4096]{2,1,0:T(8,128)(2,1)S(1)}, bf16[2,64,4096]{2,1,0:T(8,128)(2,1)}, u32[]{:S(2)}) copy-start(bf16[2,64,4096]{2,1,0:T(8,128)(2,1)} %param.24) | copy-start | bytes 3145732
  61.1 7.5 %collective-permute-start = (bf16[32,4,128,128]{3,1,2,0:T(4,128)(2,1)}, bf16[32,4,128,128]{3,1,2,0:T(4,128)(2,1)}, u32[]{:S(2)}, u32[]{:S(2)}) collective-permute-start(bf16[32,4,128,128]{3,1,2,0:T(4,128)(2,1)} %all_to_all.10), channel_id=1, source_target_pairs={{0,1},{1,0},{2,3},{3,2},{4,5},{5,4},{6,7},{7,6},{8,9},{9,8},{10,11... | collective-permute-start | bytes 12582920 | tf_op jit(solution)/shard_map/ppermute | solution.py:47
  94.0 22.7 %copy-start.13 = (f32[1,4096]{1,0:T(1,128)S(1)}, f32[1,4096]{1,0:T(1,128)}, u32[]{:S(2)}) copy-start(f32[1,4096]{1,0:T(1,128)} %param.26) | copy-start | bytes 49156
  131.7 1.3 copy-start.10
  133.1 24.5 %copy-start = (bf16[128,4096]{1,0:T(8,128)(2,1)}, bf16[128,4096]{1,0:T(8,128)(2,1)S(1)}, u32[]{:S(2)}) copy-start(bf16[128,4096]{1,0:T(8,128)(2,1)S(1)} %get-tuple-element.128) | copy-start | bytes 3145732
  133.1 24.3 %collective-permute-start.1 = (bf16[128,4096]{1,0:T(8,128)(2,1)S(1)}, bf16[128,4096]{1,0:T(8,128)(2,1)}, u32[]{:S(2)}, u32[]{:S(2)}) collective-permute-start(bf16[128,4096]{1,0:T(8,128)(2,1)S(1)} %get-tuple-element.128), channel_id=1, source_target_pairs={{0,64},{1,65},{2,66},{3,67},{4,68},{5,69},{6,70},{7,71},{8,72},{9,... | collective-permute-start | bytes 3145736 | tf_op jit(solution)/shard_map/ppermute | solution.py:127
  160.7 1.0 copy-start.11
  160.8 1.0 collective-permute-start.2
  163.1 5.5 copy-start.15
  163.1 5.6 copy-start.5
  166.8 3.4 collective-permute-start.3
  172.9 2.7 copy-start.2
  176.7 1.7 collective-permute-start.4
  182.6 1.6 collective-permute-start.5
  188.3 229.1 %collective-permute-start.6 = (bf16[128,4096]{1,0:T(8,128)(2,1)}, bf16[128,4096]{1,0:T(8,128)(2,1)}, u32[]{:S(2)}, u32[]{:S(2)}) collective-permute-start(bf16[128,4096]{1,0:T(8,128)(2,1)} %get-tuple-element.138), channel_id=1, source_target_pairs={{64,0},{65,1},{66,2},{67,3},{68,4},{69,5},{70,6},{71,7},{72,8},{73... | collective-permute-start | bytes 3145736 | tf_op jit(solution)/shard_map/ppermute | solution.py:174
  191.3 226.1 %copy-start.6 = (bf16[2,64,4096]{2,1,0:T(8,128)(2,1)S(1)}, bf16[2,64,4096]{2,1,0:T(8,128)(2,1)}, u32[]{:S(2)}) copy-start(bf16[2,64,4096]{2,1,0:T(8,128)(2,1)} %param.25) | copy-start | bytes 3145732
  422.4 16.8 %copy-start.8 = (bf16[128,4096]{1,0:T(8,128)(2,1)}, bf16[128,4096]{1,0:T(8,128)(2,1)S(1)}, u32[]{:S(2)}) copy-start(bf16[128,4096]{1,0:T(8,128)(2,1)S(1)} %get-tuple-element.257) | copy-start | bytes 3145732 | tf_op jit(solution)/shard_map/cond
  439.2 3.0 copy-start.9
  446.9 6.5 copy-start.7
  460.1 13.5 %collective-permute-start.7 = (f32[32,4,128,128]{2,3,1,0:T(8,128)}, f32[32,4,128,128]{2,3,1,0:T(8,128)}, u32[]{:S(2)}, u32[]{:S(2)}) collective-permute-start(f32[32,4,128,128]{2,3,1,0:T(8,128)} %fusion.62), channel_id=1, source_target_pairs={{0,1},{1,0},{2,3},{3,2},{4,5},{5,4},{6,7},{7,6},{8,9},{9,8},{10,11... | collective-permute-start | bytes 25165832 | tf_op jit(solution)/shard_map/ppermute | solution.py:37
  482.9 33.4 %copy-start.1 = (bf16[128,4096]{1,0:T(8,128)(2,1)S(1)}, bf16[128,4096]{1,0:T(8,128)(2,1)}, u32[]{:S(2)}) copy-start(bf16[128,4096]{1,0:T(8,128)(2,1)} %copy-done) | copy-start | bytes 3145732
  482.9 33.4 %copy-start.3 = (bf16[128,4096]{1,0:T(8,128)(2,1)S(1)}, bf16[128,4096]{1,0:T(8,128)(2,1)}, u32[]{:S(2)}) copy-start(bf16[128,4096]{1,0:T(8,128)(2,1)} %copy-done.2) | copy-start | bytes 3145732
  482.9 33.4 %copy-start.12 = (bf16[128,4096]{1,0:T(8,128)(2,1)S(1)}, bf16[128,4096]{1,0:T(8,128)(2,1)}, u32[]{:S(2)}) copy-start(bf16[128,4096]{1,0:T(8,128)(2,1)} %copy-done.11) | copy-start | bytes 3145732
  482.9 176.6 %all-to-all-start.1 = ((f32[32,4,128,128]{2,3,1,0:T(8,128)}), f32[32,4,128,128]{2,3,1,0:T(8,128)}, u32[]{:S(2)}, u32[]{:S(2)}) async-start(f32[32,4,128,128]{2,3,1,0:T(8,128)} %bitcast_add_fusion), calls=%async_computation.1 | async-start | bytes 16777216 | tf_op jit(solution)/shard_map/all_to_all | solution.py:39

commit v4 on v3

--- a/solution.py
+++ b/solution.py
@@ -98,6 +98,23 @@
         pre_act = jnp.dot(hidden, dense, preferred_element_type=jnp.float32)
         return ((values + jax.nn.silu(pre_act)).astype(jnp.bfloat16), pre_act, hidden)
 
+    def first_forward(section_input):
+        values, inv_rms, unit_rows, hidden = normalize(section_input, section_gain)
+        tile_parts = jnp.einsum(
+            "trk,rjkn->trjn",
+            hidden.reshape(row_count, blocks, TILE),
+            tile_grid,
+            preferred_element_type=jnp.float32,
+        )
+        pre_act = jnp.einsum(
+            "trjn,rjc->tcn",
+            tile_parts,
+            onehot.astype(jnp.float32),
+            precision=lax.Precision.HIGHEST,
+            preferred_element_type=jnp.float32,
+        ).reshape(row_count, model_width)
+        return ((values + jax.nn.silu(pre_act)).astype(jnp.bfloat16), pre_act, hidden)
+
     def skip_forward(section_input):
         return (
             section_input,
@@ -112,7 +129,7 @@
         first_input = lax.dynamic_index_in_dim(acts_in, micro_slot, 0, keepdims=False)
         section_input = jnp.where(section_here == 0, first_input, received)
         section_result, pre_act, hidden = lax.cond(
-            is_live, run_forward, skip_forward, section_input
+            is_live, first_forward if clock_tick == 0 else run_forward, skip_forward, section_input
         )
         section_out = store_slot(section_out, section_result, micro_slot, is_live)
         saved_inputs = store_slot(saved_inputs, section_input, micro_slot, is_live)

time: 673 us -> 643 us (0.955)
  waiting for transfers between devices: 396 us -> 359 us
  matrix products: 63 us -> 71 us
    ppermute x3, waiting for transfers between devices: 22.1 us -> 0.01 us  [run_pipeline(): received = lax.ppermute(section_result, 'pipe', pairs)]
    ppermute x3, waiting for transfers between devices: 225 us -> 211 us  [run_pipeline(): received = lax.ppermute(input_delta, 'pipe', pairs)]
    dot_general x1 -> x2, matrix products: 13.5 us -> 21.6 us  [the longest x1 15.6 us: first_forward(): jnp.einsum('trjn,rjc->tcn', tile_parts, onehot.astype(jnp.float32), preci...]
  transfers between devices with their start and end apart: 9 -> 9, of which waited for: 5 -> 4; matrix products, arithmetic and copies ran while one was open for 3% -> 9% of each run, Pallas kernels for 0% -> 0%
where the time goes in v4:
time: 643 us; the launch traced here: 638 us
  waiting for transfers between devices  359 us (56%)
  matrix products  71 us (11%)
  local copies, waits for them, and re-layouts  61.8 us (10%)
  blocking collectives  57.5 us (9%)
  other arithmetic  45.2 us (7%)
  starting transfers between devices  39.9 us (6%)
    ppermute x3, waiting for transfers between devices, run_pipeline(): received = lax.ppermute(input_delta, 'pipe', pairs)  211 us
    all_to_all x1, waiting for transfers between devices, reduce_tiles(): spread = lax.all_to_all(keep + got, ('dq', 'zl'), 0, 0, tiled=True)  139 us
    all_to_all x1, blocking collectives, gather_tiles(): mine = lax.all_to_all(sent, ('dq', 'zl'), 0, 0, tiled=True)  57.5 us
    all_to_all x1, starting transfers between devices, reduce_tiles(): spread = lax.all_to_all(keep + got, ('dq', 'zl'), 0, 0, tiled=True)  30.7 us
    unnamed x32, local copies, waits for them, and re-layouts  25.3 us
    gather x4, local copies, waits for them, and re-layouts, tile_sums(): picked = jnp.take(delta_rows, columns, axis=1)  19 us
    dot_general x1, matrix products, run_pipeline(): jnp.einsum('rjkn,rjc->rkcn', tile_grid, onehot, preferred_element_type=jn...  16.8 us
    dot_general x1, matrix products, run_backward(): lax.dot_general(pre_delta, dense, (((1,), (1,)), ((), ())), preferred_ele...  16.8 us
  transfers between devices with their start and end apart: 9, of which 4 were waited for; matrix products, arithmetic and copies ran while one was open for 9% of the time, Pallas kernels for 0%

profile of v4, /device:TPU:10, one launch (start us, length us, event | category | flops | bytes accessed | tf_op | source)
XLA Modules:
  0.0 637.7 jit_solution(14528043866486162736)
XLA Ops:
  0.6 1.0 copy.113
  1.6 1.9 broadcast_in_dim.76
  3.6 57.5 %all_to_all.10 = bf16[32,4,128,128]{3,1,2,0:T(4,128)(2,1)} all-to-all(bf16[32,4,128,128]{3,1,2,0:T(4,128)(2,1)S(1)} %broadcast_in_dim.76), channel_id=1, replica_groups=mesh['pipe'=4,'dq'=16,'zl'=2,'core'=2] {'dq','zl'}, dimensions={0} | all-to-all | bytes 8388608 | tf_op jit(solution)/shard_map/all_to_all | solution.py:46
  61.6 0.7 reduce.3
  62.5 0.6 gather_fusion
  63.4 5.1 collective-permute-done
  68.6 8.5 %pad_maximum_fusion = bf16[32,2,4,128,128]{4,2,1,3,0:T(4,128)(2,1)} fusion(bf16[32,1,4,128,128]{4,2,1,3,0:T(4,128)(2,1)} %bitcast.18, bf16[32,1,4,128,128]{4,2,1,3,0:T(4,128)(2,1)} %bitcast.17), kind=kLoop, calls=%fused_computation.108 | loop fusion | flops 4194304 | bytes 16777216 | tf_op jit(solution)/shard_map/stack | solution.py:48
  77.1 29.2 %conditional.8 = (bf16[128,4096]{1,0:T(8,128)(2,1)}, f32[128,4096]{1,0:T(8,128)}, bf16[128,4096]{1,0:T(8,128)(2,1)}) conditional(s32[]{:T(128)} %convert_element_type.149, bf16[128,4096]{1,0:T(8,128)(2,1)S(1)} %bitcast_select_fusion.3, (bf16[128,4096]{1,0:T(8,128)(2,1)S(1)}, f32[1,4096]{1,0:T(1,128)S(1)}, bf16[32,8,128,128]{3,1,2,0:T(8,128)(2,1)}, ...), branch_computations={%region_0.1_spmd, %region_1.3_spmd} | conditional | flops 2693791744 | bytes 58771992 | solution.py:131
  78.4 1.2 copy.139
  79.6 6.1 convolution_bitcast_fusion
  85.6 15.6 %fusion = f32[128,128,32,1]{1,2,3,0:T(8,128)S(1)} fusion(f32[128,32,8,128]{3,0,2,1:T(8,128)S(1)} %convolution_bitcast_fusion, bf16[32,8,32]{0,2,1:T(8,128)(2,1)S(1)} %get-tuple-element.78), kind=kOutput, calls=%fused_computation.3 | convolution fusion | flops 1610612736 | bytes 18890752 | tf_op jit(solution)/shard_map/cond/branch_1_fun/trjn,rjc->tcn/dot_general | solution.py:109
  101.2 3.6 fusion.6
  104.8 1.3 fusion.5
  106.3 1.4 collective-permute-start.1
  107.7 16.8 %convolution_convert_fusion = bf16[32,32,128,128]{3,1,2,0:T(8,128)(2,1)} fusion(pred[32,8,32,1]{2,1,3,0:T(8,128)(4,1)S(1)} %copy.128, bf16[32,8,128,128]{3,1,2,0:T(8,128)(2,1)} %bitcast.115), kind=kOutput, calls=%fused_computation.107 | convolution fusion | flops 285212672 | bytes 41951232 | tf_op jit(solution)/shard_map/rjkn,rjc->rkcn/dot_general | solution.py:86
  124.4 22.6 %copy.156 = bf16[512,8,32,128]{3,1,2,0:T(8,128)(2,1)} copy(bf16[512,8,32,128]{3,2,1,0:T(8,128)(2,1)} %bitcast.113) | data formatting | bytes 67108864
  147.3 2.9 conditional.9
  147.4 1.6 broadcast.316
  149.0 1.1 broadcast.317
  150.1 1.6 collective-permute-start.2
  152.0 4.0 conditional.10
  152.0 1.0 copy.169
  153.1 1.5 broadcast.320
  154.6 1.1 broadcast.321
  156.1 1.6 collective-permute-start.3
  157.8 1.3 broadcast_select_fusion.3
  159.2 1.4 select_select_fusion.3
  160.6 1.3 conditional.11
  160.8 1.1 broadcast.325
  161.9 2.7 select_select_fusion
  164.6 1.2 conditional.12
  164.6 1.1 broadcast.328
  165.8 1.7 collective-permute-start.4
  167.5 3.0 broadcast_select_fusion.2
  170.4 1.1 conditional.13
  170.4 1.1 broadcast.332
  171.5 1.6 collective-permute-start.5
  173.2 3.0 broadcast_select_fusion.1
  176.1 1.3 conditional.14
  176.1 1.1 broadcast.336
  177.4 1.3 collective-permute-start.6
  179.0 1.4 select_bitcast_fusion
  180.4 1.2 copy.142
  181.6 211.3 %collective-permute-done.6 = bf16[128,4096]{1,0:T(8,128)(2,1)} collective-permute-done((bf16[128,4096]{1,0:T(8,128)(2,1)}, bf16[128,4096]{1,0:T(8,128)(2,1)}, u32[]{:S(2)}, u32[]{:S(2)}) %collective-permute-start.6) | collective-permute-done | bytes 1048608 | tf_op jit(solution)/shard_map/ppermute | solution.py:191
  392.9 2.7 broadcast_select_fusion
  395.5 22.3 %conditional.15 = (bf16[128,4096]{1,0:T(8,128)(2,1)}, bf16[128,4096]{1,0:T(8,128)(2,1)S(1)}) conditional(s32[]{:T(128)} %convert_element_type.153, bf16[128,4096]{1,0:T(8,128)(2,1)} %broadcast_select_fusion, (bf16[128,4096]{1,0:T(8,128)(2,1)}, bf16[128,4096]{1,0:T(8,128)(2,1)S(1)}, f32[128,4096]{1,0:T(8,128)S(1)}, bf16[4096,4096]{1,0:T(8,128)(2,1)}, ...), branch_computations={%region_24.25_spmd, %region_25.28_spmd} | conditional | flops 4308598784 | bytes 56644168 | solution.py:180
  395.5 2.2 fusion.54
  397.8 16.8 %fusion.50 = (f32[128]{0:T(128)S(1)}, f32[128,4096]{1,0:T(8,128)S(1)}) fusion(bf16[128,4096]{1,0:T(8,128)(2,1)S(1)} %get-tuple-element.104, f32[128]{0:T(128)S(1)} %add_rsqrt_fusion.7, f32[4096]{0:T(1024)S(1)} %bitcast.131, bf16[128,4096]{1,0:T(8,128)(2,1)S(1)} %get-tuple-element.279, bf16[4096,4096]{1,0:T(8,128)(2,1)} %get-tuple-element.106), kind=kOutput, calls=%fused_computation.97 | convolution fusion | flops 4297588736 | bytes 37766144 | tf_op jit(solution)/shard_map/cond/branch_1_fun/dot_general | solution.py:153
  414.6 3.0 fusion.55
  418.2 0.7 copy.118
  418.8 0.7 copy.119
  419.5 3.0 gather_fusion.2
  422.5 6.5 %copy.123 = bf16[32,4,128,128]{2,3,1,0:T(8,128)(2,1)} copy(bf16[32,4,128,128]{3,2,1,0:T(8,128)(2,1)} %bitcast.117) | data formatting | bytes 8388608 | tf_op jit(solution)/shard_map/jit(_take)/gather | solution.py:33
  429.0 6.7 %fusion.67 = f32[32,4,128,128]{2,3,1,0:T(8,128)} fusion(bf16[32,4,128,128]{2,3,1,0:T(8,128)(2,1)} %copy.123, pred[32,4]{1,0:T(8,128)(4,1)S(1)} %get-tuple-element.236, bf16[128,32,128,1]{2,1,0,3:T(8,128)(2,1)S(1)} %bitcast.118), kind=kOutput, calls=%fused_computation.118 | convolution fusion | flops 538968064 | bytes 13631616 | tf_op jit(solution)/shard_map/trk,trjn->rjkn/dot_general | solution.py:34
  435.9 3.1 gather_fusion.1
  438.9 6.4 %copy.120 = bf16[32,4,128,128]{2,3,1,0:T(8,128)(2,1)} copy(bf16[32,4,128,128]{3,2,1,0:T(8,128)(2,1)} %bitcast.116) | data formatting | bytes 8388608 | tf_op jit(solution)/shard_map/jit(_take)/gather | solution.py:33
  445.4 3.9 collective-permute-done.7
  449.3 9.2 %bitcast_add_fusion = f32[32,4,128,128]{2,3,1,0:T(8,128)} fusion(f32[32,4,128,128]{2,3,1,0:T(8,128)} %collective-permute-done.7, bf16[32,4,128,128]{2,3,1,0:T(8,128)(2,1)} %copy.120, pred[32,4]{1,0:T(8,128)(4,1)S(1)} %get-tuple-element.208, bf16[128,32,128,1]{2,1,0,3:T(8,128)(2,1)S(1)} %bitcast.119), kind=kOutput, calls=%fused_computation.109 | convolution fusion | flops 541065216 | bytes 22020224 | tf_op jit(solution)/shard_map/trk,trjn->rjkn/dot_general | solution.py:34
  458.5 30.7 %all-to-all-start.1 = ((f32[32,4,128,128]{2,3,1,0:T(8,128)}), f32[32,4,128,128]{2,3,1,0:T(8,128)}, u32[]{:S(2)}, u32[]{:S(2)}) async-start(f32[32,4,128,128]{2,3,1,0:T(8,128)} %bitcast_add_fusion), calls=%async_computation.1 | async-start | bytes 16777216 | tf_op jit(solution)/shard_map/all_to_all | solution.py:39
  489.2 2.4 select_select_fusion.4
  491.6 2.4 select_select_fusion.2
  493.9 138.9 %all-to-all-done.1 = f32[32,4,128,128]{2,3,1,0:T(8,128)} async-done(((f32[32,4,128,128]{2,3,1,0:T(8,128)}), f32[32,4,128,128]{2,3,1,0:T(8,128)}, u32[]{:S(2)}, u32[]{:S(2)}) %all-to-all-start.1) | async-done | bytes 8388640 | tf_op jit(solution)/shard_map/all_to_all | solution.py:39
  632.8 3.8 reduce_sum.117
  636.6 0.8 copy.125
  (66 shorter events, 3.3 us)
Async XLA Ops:
  3.5 58.1 %copy-start.14 = (s32[1,256]{1,0:T(1,128)S(1)}, s32[1,256]{1,0:T(1,128)}, u32[]{:S(2)}) copy-start(s32[1,256]{1,0:T(1,128)} %param.28) | copy-start | bytes 3076
  3.5 59.8 %copy-start.2 = (bf16[2,64,4096]{2,1,0:T(8,128)(2,1)S(1)}, bf16[2,64,4096]{2,1,0:T(8,128)(2,1)}, u32[]{:S(2)}) copy-start(bf16[2,64,4096]{2,1,0:T(8,128)(2,1)} %param.24) | copy-start | bytes 3145732
  61.1 7.5 %collective-permute-start = (bf16[32,4,128,128]{3,1,2,0:T(4,128)(2,1)}, bf16[32,4,128,128]{3,1,2,0:T(4,128)(2,1)}, u32[]{:S(2)}, u32[]{:S(2)}) collective-permute-start(bf16[32,4,128,128]{3,1,2,0:T(4,128)(2,1)} %all_to_all.10), channel_id=1, source_target_pairs={{0,1},{1,0},{2,3},{3,2},{4,5},{5,4},{6,7},{7,6},{8,9},{9,8},{10,11... | collective-permute-start | bytes 12582920 | tf_op jit(solution)/shard_map/ppermute | solution.py:47
  62.4 14.8 %copy-start.12 = (s32[32,8]{1,0:T(8,128)}, s32[32,8]{1,0:T(8,128)S(1)}, u32[]{:S(2)}) copy-start(s32[32,8]{1,0:T(8,128)S(1)} %reshape_squeeze.3) | copy-start | bytes 3076
  68.6 8.6 %copy-start.11 = (f32[1,4096]{1,0:T(1,128)S(1)}, f32[1,4096]{1,0:T(1,128)}, u32[]{:S(2)}) copy-start(f32[1,4096]{1,0:T(1,128)} %param.26) | copy-start | bytes 49156
  106.3 40.8 %collective-permute-start.1 = (bf16[128,4096]{1,0:T(8,128)(2,1)}, bf16[128,4096]{1,0:T(8,128)(2,1)S(1)}, u32[]{:S(2)}, u32[]{:S(2)}) collective-permute-start(bf16[128,4096]{1,0:T(8,128)(2,1)} %get-tuple-element.131), channel_id=1, source_target_pairs={{0,64},{1,65},{2,66},{3,67},{4,68},{5,69},{6,70},{7,71},{8,72},{9,... | collective-permute-start | bytes 3145736 | tf_op jit(solution)/shard_map/ppermute | solution.py:144
  147.3 4.5 copy-start.3
  150.1 1.7 copy-start.9
  150.1 1.7 collective-permute-start.2
  152.0 5.7 copy-start.15
  152.0 5.8 copy-start.4
  156.1 3.1 collective-permute-start.3
  161.9 2.7 copy-start
  165.8 1.7 collective-permute-start.4
  171.5 1.6 collective-permute-start.5
  176.1 2.6 copy-start.13
  177.4 215.4 %collective-permute-start.6 = (bf16[128,4096]{1,0:T(8,128)(2,1)}, bf16[128,4096]{1,0:T(8,128)(2,1)}, u32[]{:S(2)}, u32[]{:S(2)}) collective-permute-start(bf16[128,4096]{1,0:T(8,128)(2,1)} %get-tuple-element.141), channel_id=1, source_target_pairs={{64,0},{65,1},{66,2},{67,3},{68,4},{69,5},{70,6},{71,7},{72,8},{73... | collective-permute-start | bytes 3145736 | tf_op jit(solution)/shard_map/ppermute | solution.py:191
  180.4 212.5 %copy-start.5 = (bf16[2,64,4096]{2,1,0:T(8,128)(2,1)S(1)}, bf16[2,64,4096]{2,1,0:T(8,128)(2,1)}, u32[]{:S(2)}) copy-start(bf16[2,64,4096]{2,1,0:T(8,128)(2,1)} %param.25) | copy-start | bytes 3145732
  397.8 16.8 %copy-start.7 = (bf16[128,4096]{1,0:T(8,128)(2,1)}, bf16[128,4096]{1,0:T(8,128)(2,1)S(1)}, u32[]{:S(2)}) copy-start(bf16[128,4096]{1,0:T(8,128)(2,1)S(1)} %get-tuple-element.279) | copy-start | bytes 3145732 | tf_op jit(solution)/shard_map/cond
  414.6 3.0 copy-start.8
  422.5 6.5 %copy-start.6 = (bf16[16,8,32,128]{3,2,1,0:T(8,128)(2,1)S(1)}, bf16[16,8,32,128]{3,2,1,0:T(8,128)(2,1)}, u32[]{:S(2)}) copy-start(bf16[16,8,32,128]{3,2,1,0:T(8,128)(2,1)} %copy.142) | copy-start | bytes 3145732
  435.8 13.5 %collective-permute-start.7 = (f32[32,4,128,128]{2,3,1,0:T(8,128)}, f32[32,4,128,128]{2,3,1,0:T(8,128)}, u32[]{:S(2)}, u32[]{:S(2)}) collective-permute-start(f32[32,4,128,128]{2,3,1,0:T(8,128)} %fusion.67), channel_id=1, source_target_pairs={{0,1},{1,0},{2,3},{3,2},{4,5},{5,4},{6,7},{7,6},{8,9},{9,8},{10,11... | collective-permute-start | bytes 25165832 | tf_op jit(solution)/shard_map/ppermute | solution.py:37
  458.5 30.7 %copy-start.1 = (bf16[128,4096]{1,0:T(8,128)(2,1)S(1)}, bf16[128,4096]{1,0:T(8,128)(2,1)}, u32[]{:S(2)}) copy-start(bf16[128,4096]{1,0:T(8,128)(2,1)} %copy-done) | copy-start | bytes 3145732
  458.5 30.7 %copy-start.10 = (bf16[128,4096]{1,0:T(8,128)(2,1)S(1)}, bf16[128,4096]{1,0:T(8,128)(2,1)}, u32[]{:S(2)}) copy-start(bf16[128,4096]{1,0:T(8,128)(2,1)} %copy-done.9) | copy-start | bytes 3145732
  458.5 174.3 %all-to-all-start.1 = ((f32[32,4,128,128]{2,3,1,0:T(8,128)}), f32[32,4,128,128]{2,3,1,0:T(8,128)}, u32[]{:S(2)}, u32[]{:S(2)}) async-start(f32[32,4,128,128]{2,3,1,0:T(8,128)} %bitcast_add_fusion), calls=%async_computation.1 | async-start | bytes 16777216 | tf_op jit(solution)/shard_map/all_to_all | solution.py:39

commit v5 on v4

--- a/solution.py
+++ b/solution.py
@@ -110,7 +110,7 @@
             "trjn,rjc->tcn",
             tile_parts,
             onehot.astype(jnp.float32),
-            precision=lax.Precision.HIGHEST,
+            precision=lax.Precision.HIGH,
             preferred_element_type=jnp.float32,
         ).reshape(row_count, model_width)
         return ((values + jax.nn.silu(pre_act)).astype(jnp.bfloat16), pre_act, hidden)

time: 643 us -> 641 us (level)
  transfers between devices with their start and end apart: 9 -> 9, of which waited for: 4 -> 4; matrix products, arithmetic and copies ran while one was open for 9% -> 10% of each run, Pallas kernels for 0% -> 0%
where the time goes in v5:
time: 641 us; the launch traced here: 635 us
  waiting for transfers between devices  358 us (56%)
  matrix products  68.5 us (11%)
  local copies, waits for them, and re-layouts  61.8 us (10%)
  blocking collectives  57.5 us (9%)
  other arithmetic  46.8 us (7%)
  starting transfers between devices  39.9 us (6%)
    ppermute x3, waiting for transfers between devices, run_pipeline(): received = lax.ppermute(input_delta, 'pipe', pairs)  211 us
    all_to_all x1, waiting for transfers between devices, reduce_tiles(): spread = lax.all_to_all(keep + got, ('dq', 'zl'), 0, 0, tiled=True)  138 us
    all_to_all x1, blocking collectives, gather_tiles(): mine = lax.all_to_all(sent, ('dq', 'zl'), 0, 0, tiled=True)  57.5 us
    all_to_all x1, starting transfers between devices, reduce_tiles(): spread = lax.all_to_all(keep + got, ('dq', 'zl'), 0, 0, tiled=True)  30.7 us
    unnamed x32, local copies, waits for them, and re-layouts  25.3 us
    gather x4, local copies, waits for them, and re-layouts, tile_sums(): picked = jnp.take(delta_rows, columns, axis=1)  19 us
    dot_general x1, matrix products, run_pipeline(): jnp.einsum('rjkn,rjc->rkcn', tile_grid, onehot, preferred_element_type=jn...  16.8 us
    dot_general x1, matrix products, run_backward(): lax.dot_general(pre_delta, dense, (((1,), (1,)), ((), ())), preferred_ele...  16.8 us
  transfers between devices with their start and end apart: 9, of which 4 were waited for; matrix products, arithmetic and copies ran while one was open for 10% of the time, Pallas kernels for 0%

profile of v5, /device:TPU:10, one launch (start us, length us, event | category | flops | bytes accessed | tf_op | source)
XLA Modules:
  0.0 635.5 jit_solution(13603275715018633983)
XLA Ops:
  0.6 1.0 copy.113
  1.6 1.9 broadcast_in_dim.76
  3.6 57.5 %all_to_all.10 = bf16[32,4,128,128]{3,1,2,0:T(4,128)(2,1)} all-to-all(bf16[32,4,128,128]{3,1,2,0:T(4,128)(2,1)S(1)} %broadcast_in_dim.76), channel_id=1, replica_groups=mesh['pipe'=4,'dq'=16,'zl'=2,'core'=2] {'dq','zl'}, dimensions={0} | all-to-all | bytes 8388608 | tf_op jit(solution)/shard_map/all_to_all | solution.py:46
  61.6 0.7 reduce.3
  62.5 0.6 gather_fusion
  63.4 5.1 collective-permute-done
  68.6 8.5 %pad_maximum_fusion = bf16[32,2,4,128,128]{4,2,1,3,0:T(4,128)(2,1)} fusion(bf16[32,1,4,128,128]{4,2,1,3,0:T(4,128)(2,1)} %bitcast.18, bf16[32,1,4,128,128]{4,2,1,3,0:T(4,128)(2,1)} %bitcast.17), kind=kLoop, calls=%fused_computation.108 | loop fusion | flops 4194304 | bytes 16777216 | tf_op jit(solution)/shard_map/stack | solution.py:48
  77.1 28.2 %conditional.8 = (bf16[128,4096]{1,0:T(8,128)(2,1)}, f32[128,4096]{1,0:T(8,128)}, bf16[128,4096]{1,0:T(8,128)(2,1)}) conditional(s32[]{:T(128)} %convert_element_type.149, bf16[128,4096]{1,0:T(8,128)(2,1)S(1)} %bitcast_select_fusion.3, (bf16[128,4096]{1,0:T(8,128)(2,1)S(1)}, f32[1,4096]{1,0:T(1,128)S(1)}, bf16[32,8,128,128]{3,1,2,0:T(8,128)(2,1)}, ...), branch_computations={%region_0.1_spmd, %region_1.3_spmd} | conditional | flops 1888485504 | bytes 58771992 | solution.py:131
  78.4 1.2 copy.139
  79.6 6.1 convolution_bitcast_fusion
  85.6 13.0 %fusion = f32[128,128,32,1]{1,2,3,0:T(8,128)} fusion(f32[128,32,8,128]{3,0,2,1:T(8,128)S(1)} %convolution_bitcast_fusion, bf16[32,8,32]{0,2,1:T(8,128)(2,1)S(1)} %get-tuple-element.78), kind=kOutput, calls=%fused_computation.3 | convolution fusion | flops 805306368 | bytes 18890752 | tf_op jit(solution)/shard_map/cond/branch_1_fun/trjn,rjc->tcn/dot_general | solution.py:109
  98.6 5.2 fusion.6
  103.8 1.3 fusion.5
  105.3 1.4 collective-permute-start.1
  106.7 16.8 %convolution_convert_fusion = bf16[32,32,128,128]{3,1,2,0:T(8,128)(2,1)} fusion(pred[32,8,32,1]{2,1,3,0:T(8,128)(4,1)S(1)} %copy.128, bf16[32,8,128,128]{3,1,2,0:T(8,128)(2,1)} %bitcast.115), kind=kOutput, calls=%fused_computation.107 | convolution fusion | flops 285212672 | bytes 41951232 | tf_op jit(solution)/shard_map/rjkn,rjc->rkcn/dot_general | solution.py:86
  123.5 22.6 %copy.156 = bf16[512,8,32,128]{3,1,2,0:T(8,128)(2,1)} copy(bf16[512,8,32,128]{3,2,1,0:T(8,128)(2,1)} %bitcast.113) | data formatting | bytes 67108864
  146.3 2.9 conditional.9
  146.4 1.6 broadcast.316
  148.0 1.1 broadcast.317
  149.2 1.6 collective-permute-start.2
  151.0 4.0 conditional.10
  151.1 1.0 copy.169
  152.1 1.5 broadcast.320
  153.6 1.1 broadcast.321
  155.1 1.6 collective-permute-start.3
  156.9 1.3 broadcast_select_fusion.3
  158.2 1.4 select_select_fusion.3
  159.6 1.3 conditional.11
  159.9 1.1 broadcast.325
  160.9 2.7 select_select_fusion
  163.6 1.2 conditional.12
  163.6 1.1 broadcast.328
  164.8 1.7 collective-permute-start.4
  166.5 3.0 broadcast_select_fusion.2
  169.5 1.1 conditional.13
  169.5 1.1 broadcast.332
  170.6 1.6 collective-permute-start.5
  172.2 3.0 broadcast_select_fusion.1
  175.1 1.3 conditional.14
  175.1 1.1 broadcast.336
  176.5 1.3 collective-permute-start.6
  178.0 1.4 select_bitcast_fusion
  179.4 1.2 copy.142
  180.6 211.2 %collective-permute-done.6 = bf16[128,4096]{1,0:T(8,128)(2,1)} collective-permute-done((bf16[128,4096]{1,0:T(8,128)(2,1)}, bf16[128,4096]{1,0:T(8,128)(2,1)}, u32[]{:S(2)}, u32[]{:S(2)}) %collective-permute-start.6) | collective-permute-done | bytes 1048608 | tf_op jit(solution)/shard_map/ppermute | solution.py:191
  391.8 2.7 broadcast_select_fusion
  394.5 22.3 %conditional.15 = (bf16[128,4096]{1,0:T(8,128)(2,1)}, bf16[128,4096]{1,0:T(8,128)(2,1)S(1)}) conditional(s32[]{:T(128)} %convert_element_type.153, bf16[128,4096]{1,0:T(8,128)(2,1)} %broadcast_select_fusion, (bf16[128,4096]{1,0:T(8,128)(2,1)}, bf16[128,4096]{1,0:T(8,128)(2,1)S(1)}, f32[128,4096]{1,0:T(8,128)S(1)}, bf16[4096,4096]{1,0:T(8,128)(2,1)}, ...), branch_computations={%region_24.25_spmd, %region_25.28_spmd} | conditional | flops 4308598784 | bytes 56644168 | solution.py:180
  394.5 2.2 fusion.54
  396.7 16.8 %fusion.50 = (f32[128]{0:T(128)S(1)}, f32[128,4096]{1,0:T(8,128)S(1)}) fusion(bf16[128,4096]{1,0:T(8,128)(2,1)S(1)} %get-tuple-element.104, f32[128]{0:T(128)S(1)} %add_rsqrt_fusion.7, f32[4096]{0:T(1024)S(1)} %bitcast.131, bf16[128,4096]{1,0:T(8,128)(2,1)S(1)} %get-tuple-element.279, bf16[4096,4096]{1,0:T(8,128)(2,1)} %get-tuple-element.106), kind=kOutput, calls=%fused_computation.97 | convolution fusion | flops 4297588736 | bytes 37766144 | tf_op jit(solution)/shard_map/cond/branch_1_fun/dot_general | solution.py:153
  413.5 3.0 fusion.55
  417.1 0.7 copy.118
  417.8 0.7 copy.119
  418.5 3.0 gather_fusion.2
  421.5 6.5 %copy.123 = bf16[32,4,128,128]{2,3,1,0:T(8,128)(2,1)} copy(bf16[32,4,128,128]{3,2,1,0:T(8,128)(2,1)} %bitcast.117) | data formatting | bytes 8388608 | tf_op jit(solution)/shard_map/jit(_take)/gather | solution.py:33
  428.0 6.7 %fusion.67 = f32[32,4,128,128]{2,3,1,0:T(8,128)} fusion(bf16[32,4,128,128]{2,3,1,0:T(8,128)(2,1)} %copy.123, pred[32,4]{1,0:T(8,128)(4,1)S(1)} %get-tuple-element.236, bf16[128,32,128,1]{2,1,0,3:T(8,128)(2,1)S(1)} %bitcast.118), kind=kOutput, calls=%fused_computation.118 | convolution fusion | flops 538968064 | bytes 13631616 | tf_op jit(solution)/shard_map/trk,trjn->rjkn/dot_general | solution.py:34
  434.9 3.1 gather_fusion.1
  437.9 6.4 %copy.120 = bf16[32,4,128,128]{2,3,1,0:T(8,128)(2,1)} copy(bf16[32,4,128,128]{3,2,1,0:T(8,128)(2,1)} %bitcast.116) | data formatting | bytes 8388608 | tf_op jit(solution)/shard_map/jit(_take)/gather | solution.py:33
  444.3 3.9 collective-permute-done.7
  448.2 9.2 %bitcast_add_fusion = f32[32,4,128,128]{2,3,1,0:T(8,128)} fusion(f32[32,4,128,128]{2,3,1,0:T(8,128)} %collective-permute-done.7, bf16[32,4,128,128]{2,3,1,0:T(8,128)(2,1)} %copy.120, pred[32,4]{1,0:T(8,128)(4,1)S(1)} %get-tuple-element.208, bf16[128,32,128,1]{2,1,0,3:T(8,128)(2,1)S(1)} %bitcast.119), kind=kOutput, calls=%fused_computation.109 | convolution fusion | flops 541065216 | bytes 22020224 | tf_op jit(solution)/shard_map/trk,trjn->rjkn/dot_general | solution.py:34
  457.5 30.7 %all-to-all-start.1 = ((f32[32,4,128,128]{2,3,1,0:T(8,128)}), f32[32,4,128,128]{2,3,1,0:T(8,128)}, u32[]{:S(2)}, u32[]{:S(2)}) async-start(f32[32,4,128,128]{2,3,1,0:T(8,128)} %bitcast_add_fusion), calls=%async_computation.1 | async-start | bytes 16777216 | tf_op jit(solution)/shard_map/all_to_all | solution.py:39
  488.2 2.4 select_select_fusion.4
  490.6 2.4 select_select_fusion.2
  493.0 137.6 %all-to-all-done.1 = f32[32,4,128,128]{2,3,1,0:T(8,128)} async-done(((f32[32,4,128,128]{2,3,1,0:T(8,128)}), f32[32,4,128,128]{2,3,1,0:T(8,128)}, u32[]{:S(2)}, u32[]{:S(2)}) %all-to-all-start.1) | async-done | bytes 8388640 | tf_op jit(solution)/shard_map/all_to_all | solution.py:39
  630.5 3.8 reduce_sum.117
  634.4 0.8 copy.125
  (66 shorter events, 3.3 us)
Async XLA Ops:
  3.5 58.1 %copy-start.14 = (s32[1,256]{1,0:T(1,128)S(1)}, s32[1,256]{1,0:T(1,128)}, u32[]{:S(2)}) copy-start(s32[1,256]{1,0:T(1,128)} %param.28) | copy-start | bytes 3076
  3.5 59.8 %copy-start.2 = (bf16[2,64,4096]{2,1,0:T(8,128)(2,1)S(1)}, bf16[2,64,4096]{2,1,0:T(8,128)(2,1)}, u32[]{:S(2)}) copy-start(bf16[2,64,4096]{2,1,0:T(8,128)(2,1)} %param.24) | copy-start | bytes 3145732
  61.1 7.5 %collective-permute-start = (bf16[32,4,128,128]{3,1,2,0:T(4,128)(2,1)}, bf16[32,4,128,128]{3,1,2,0:T(4,128)(2,1)}, u32[]{:S(2)}, u32[]{:S(2)}) collective-permute-start(bf16[32,4,128,128]{3,1,2,0:T(4,128)(2,1)} %all_to_all.10), channel_id=1, source_target_pairs={{0,1},{1,0},{2,3},{3,2},{4,5},{5,4},{6,7},{7,6},{8,9},{9,8},{10,11... | collective-permute-start | bytes 12582920 | tf_op jit(solution)/shard_map/ppermute | solution.py:47
  62.4 14.8 %copy-start.12 = (s32[32,8]{1,0:T(8,128)}, s32[32,8]{1,0:T(8,128)S(1)}, u32[]{:S(2)}) copy-start(s32[32,8]{1,0:T(8,128)S(1)} %reshape_squeeze.3) | copy-start | bytes 3076
  68.6 8.6 %copy-start.11 = (f32[1,4096]{1,0:T(1,128)S(1)}, f32[1,4096]{1,0:T(1,128)}, u32[]{:S(2)}) copy-start(f32[1,4096]{1,0:T(1,128)} %param.26) | copy-start | bytes 49156
  105.3 40.8 %collective-permute-start.1 = (bf16[128,4096]{1,0:T(8,128)(2,1)}, bf16[128,4096]{1,0:T(8,128)(2,1)S(1)}, u32[]{:S(2)}, u32[]{:S(2)}) collective-permute-start(bf16[128,4096]{1,0:T(8,128)(2,1)} %get-tuple-element.131), channel_id=1, source_target_pairs={{0,64},{1,65},{2,66},{3,67},{4,68},{5,69},{6,70},{7,71},{8,72},{9,... | collective-permute-start | bytes 3145736 | tf_op jit(solution)/shard_map/ppermute | solution.py:144
  146.3 4.5 copy-start.3
  149.2 1.7 copy-start.9
  149.2 1.7 collective-permute-start.2
  151.0 5.7 copy-start.15
  151.0 5.8 copy-start.4
  155.1 3.1 collective-permute-start.3
  160.9 2.7 copy-start
  164.8 1.7 collective-permute-start.4
  170.6 1.6 collective-permute-start.5
  175.1 2.6 copy-start.13
  176.5 215.4 %collective-permute-start.6 = (bf16[128,4096]{1,0:T(8,128)(2,1)}, bf16[128,4096]{1,0:T(8,128)(2,1)}, u32[]{:S(2)}, u32[]{:S(2)}) collective-permute-start(bf16[128,4096]{1,0:T(8,128)(2,1)} %get-tuple-element.141), channel_id=1, source_target_pairs={{64,0},{65,1},{66,2},{67,3},{68,4},{69,5},{70,6},{71,7},{72,8},{73... | collective-permute-start | bytes 3145736 | tf_op jit(solution)/shard_map/ppermute | solution.py:191
  179.4 212.4 %copy-start.5 = (bf16[2,64,4096]{2,1,0:T(8,128)(2,1)S(1)}, bf16[2,64,4096]{2,1,0:T(8,128)(2,1)}, u32[]{:S(2)}) copy-start(bf16[2,64,4096]{2,1,0:T(8,128)(2,1)} %param.25) | copy-start | bytes 3145732
  396.7 16.8 %copy-start.7 = (bf16[128,4096]{1,0:T(8,128)(2,1)}, bf16[128,4096]{1,0:T(8,128)(2,1)S(1)}, u32[]{:S(2)}) copy-start(bf16[128,4096]{1,0:T(8,128)(2,1)S(1)} %get-tuple-element.279) | copy-start | bytes 3145732 | tf_op jit(solution)/shard_map/cond
  413.5 3.0 copy-start.8
  421.5 6.5 %copy-start.6 = (bf16[16,8,32,128]{3,2,1,0:T(8,128)(2,1)S(1)}, bf16[16,8,32,128]{3,2,1,0:T(8,128)(2,1)}, u32[]{:S(2)}) copy-start(bf16[16,8,32,128]{3,2,1,0:T(8,128)(2,1)} %copy.142) | copy-start | bytes 3145732
  434.7 13.5 %collective-permute-start.7 = (f32[32,4,128,128]{2,3,1,0:T(8,128)}, f32[32,4,128,128]{2,3,1,0:T(8,128)}, u32[]{:S(2)}, u32[]{:S(2)}) collective-permute-start(f32[32,4,128,128]{2,3,1,0:T(8,128)} %fusion.67), channel_id=1, source_target_pairs={{0,1},{1,0},{2,3},{3,2},{4,5},{5,4},{6,7},{7,6},{8,9},{9,8},{10,11... | collective-permute-start | bytes 25165832 | tf_op jit(solution)/shard_map/ppermute | solution.py:37
  457.4 30.7 %copy-start.1 = (bf16[128,4096]{1,0:T(8,128)(2,1)S(1)}, bf16[128,4096]{1,0:T(8,128)(2,1)}, u32[]{:S(2)}) copy-start(bf16[128,4096]{1,0:T(8,128)(2,1)} %copy-done) | copy-start | bytes 3145732
  457.4 30.7 %copy-start.10 = (bf16[128,4096]{1,0:T(8,128)(2,1)S(1)}, bf16[128,4096]{1,0:T(8,128)(2,1)}, u32[]{:S(2)}) copy-start(bf16[128,4096]{1,0:T(8,128)(2,1)} %copy-done.9) | copy-start | bytes 3145732
  457.5 173.1 %all-to-all-start.1 = ((f32[32,4,128,128]{2,3,1,0:T(8,128)}), f32[32,4,128,128]{2,3,1,0:T(8,128)}, u32[]{:S(2)}, u32[]{:S(2)}) async-start(f32[32,4,128,128]{2,3,1,0:T(8,128)} %bitcast_add_fusion), calls=%async_computation.1 | async-start | bytes 16777216 | tf_op jit(solution)/shard_map/all_to_all | solution.py:39

commit v6 on v3

--- a/solution.py
+++ b/solution.py
@@ -45,7 +45,7 @@
     sent = jnp.broadcast_to(shard[None], (chips,) + shard.shape)
     mine = lax.all_to_all(sent, ("dq", "zl"), 0, 0, tiled=True)
     other = lax.ppermute(mine, "core", [(0, 1), (1, 0)])
-    return jnp.stack([mine, other], 1).reshape((-1,) + shard.shape[1:])
+    return mine, other
 
 
 def on_device(acts_in, cotangent, norm_gains, weights, tile_columns, lengths):
@@ -76,8 +76,8 @@
     section_gain = norm_gains[0]
     column_list = tile_columns[0]
     column_table = column_list.reshape(blocks, KEEP)
-    gathered = gather_tiles(weights[0])
-    tile_grid = gathered.reshape(blocks, KEEP, TILE, TILE)
+    mine, other = gather_tiles(weights[0])
+    tile_grid = jnp.stack([mine, other], 1).reshape(blocks, KEEP, TILE, TILE)
     core = lax.axis_index("core")
     local_order = (jnp.arange(KEEP, dtype=jnp.int32) + (KEEP // 2) * core) % KEEP
     local_table = jnp.take(column_table, local_order, axis=1)
@@ -98,6 +98,27 @@
         pre_act = jnp.dot(hidden, dense, preferred_element_type=jnp.float32)
         return ((values + jax.nn.silu(pre_act)).astype(jnp.bfloat16), pre_act, hidden)
 
+    def first_forward(section_input):
+        values, inv_rms, unit_rows, hidden = normalize(section_input, section_gain)
+        half = KEEP // 2
+        pre_act = 0.0
+        for tiles, picks in ((mine, onehot[:, :half]), (other, onehot[:, half:])):
+            tile_parts = jnp.einsum(
+                "trk,rjkn->trjn",
+                hidden.reshape(row_count, blocks, TILE),
+                tiles,
+                preferred_element_type=jnp.float32,
+            )
+            pre_act = pre_act + jnp.einsum(
+                "trjn,rjc->tcn",
+                tile_parts,
+                picks.astype(jnp.float32),
+                precision=lax.Precision.HIGHEST,
+                preferred_element_type=jnp.float32,
+            )
+        pre_act = pre_act.reshape(row_count, model_width)
+        return ((values + jax.nn.silu(pre_act)).astype(jnp.bfloat16), pre_act, hidden)
+
     def skip_forward(section_input):
         return (
             section_input,
@@ -112,7 +133,7 @@
         first_input = lax.dynamic_index_in_dim(acts_in, micro_slot, 0, keepdims=False)
         section_input = jnp.where(section_here == 0, first_input, received)
         section_result, pre_act, hidden = lax.cond(
-            is_live, run_forward, skip_forward, section_input
+            is_live, first_forward if clock_tick == 0 else run_forward, skip_forward, section_input
         )
         section_out = store_slot(section_out, section_result, micro_slot, is_live)
         saved_inputs = store_slot(saved_inputs, section_input, micro_slot, is_live)

time: 673 us -> 642 us (0.954)
  waiting for transfers between devices: 396 us -> 348 us
  local copies, waits for them, and re-layouts: 62.1 us -> 72.4 us
  matrix products: 63 us -> 72.5 us
    ppermute x3, waiting for transfers between devices: 22.1 us -> 0.01 us  [run_pipeline(): received = lax.ppermute(section_result, 'pipe', pairs)]
    ppermute x3, waiting for transfers between devices: 225 us -> 207 us  [run_pipeline(): received = lax.ppermute(input_delta, 'pipe', pairs)]
    another operation x9 -> x10, local copies, waits for them, and re-layouts: 9.84 us -> 20.9 us  [the longest x1 11.1 us: run_pipeline(): tile_grid = jnp.stack([mine, other], 1).reshape(blocks, KEEP, TILE, TILE)]
    dot_general x1 -> x4, matrix products: 13.5 us -> 23.1 us  [the longest x2 16.2 us: first_forward(): jnp.einsum('trjn,rjc->tcn', tile_parts, picks.astype(jnp.float32), precis...]
    all_to_all x1, waiting for transfers between devices: 140 us -> 132 us  [reduce_tiles(): spread = lax.all_to_all(keep + got, ('dq', 'zl'), 0, 0, tiled=True)]
    unnamed x32 -> x34, local copies, waits for them, and re-layouts: 26.8 us -> 26.6 us
  transfers between devices with their start and end apart: 9 -> 9, of which waited for: 5 -> 4; matrix products, arithmetic and copies ran while one was open for 3% -> 12% of each run, Pallas kernels for 0% -> 0%
where the time goes in v6:
time: 642 us; the launch traced here: 638 us
  waiting for transfers between devices  348 us (54%)
  matrix products  72.5 us (11%)
  local copies, waits for them, and re-layouts  72.4 us (11%)
  blocking collectives  57.5 us (9%)
  other arithmetic  43.6 us (7%)
  starting transfers between devices  41.3 us (6%)
    ppermute x3, waiting for transfers between devices, run_pipeline(): received = lax.ppermute(input_delta, 'pipe', pairs)  207 us
    all_to_all x1, waiting for transfers between devices, reduce_tiles(): spread = lax.all_to_all(keep + got, ('dq', 'zl'), 0, 0, tiled=True)  132 us
    all_to_all x1, blocking collectives, gather_tiles(): mine = lax.all_to_all(sent, ('dq', 'zl'), 0, 0, tiled=True)  57.5 us
    all_to_all x1, starting transfers between devices, reduce_tiles(): spread = lax.all_to_all(keep + got, ('dq', 'zl'), 0, 0, tiled=True)  31.8 us
    unnamed x34, local copies, waits for them, and re-layouts  26.6 us
    gather x4, local copies, waits for them, and re-layouts, tile_sums(): picked = jnp.take(delta_rows, columns, axis=1)  19.2 us
    dot_general x1, matrix products, run_pipeline(): jnp.einsum('rjkn,rjc->rkcn', tile_grid, onehot, preferred_element_type=jn...  16.8 us
    dot_general x1, matrix products, run_backward(): lax.dot_general(pre_delta, dense, (((1,), (1,)), ((), ())), preferred_ele...  16.7 us
  transfers between devices with their start and end apart: 9, of which 4 were waited for; matrix products, arithmetic and copies ran while one was open for 12% of the time, Pallas kernels for 0%

profile of v6, /device:TPU:10, one launch (start us, length us, event | category | flops | bytes accessed | tf_op | source)
XLA Modules:
  0.0 638.3 jit_solution(4210037338192062300)
XLA Ops:
  0.6 1.9 broadcast_in_dim.76
  2.6 57.5 %all_to_all.10 = bf16[32,4,128,128]{3,2,1,0:T(8,128)(2,1)} all-to-all(bf16[32,4,128,128]{3,2,1,0:T(8,128)(2,1)S(1)} %broadcast_in_dim.76), channel_id=1, replica_groups=mesh['pipe'=4,'dq'=16,'zl'=2,'core'=2] {'dq','zl'}, dimensions={0} | all-to-all | bytes 8388608 | tf_op jit(solution)/shard_map/all_to_all | solution.py:46
  60.7 0.7 reduce.3
  62.5 5.1 collective-permute-done
  67.6 29.5 %conditional.8 = (bf16[128,4096]{1,0:T(8,128)(2,1)}, f32[128,4096]{1,0:T(8,128)}, bf16[128,4096]{1,0:T(8,128)(2,1)}) conditional(s32[]{:T(128)} %convert_element_type.150, bf16[128,4096]{1,0:T(8,128)(2,1)S(1)} %bitcast_select_fusion.3, (bf16[128,4096]{1,0:T(8,128)(2,1)S(1)}, f32[1,4096]{1,0:T(1,128)S(1)}, bf16[32,4,128,128]{3,2,1,0:T(8,128)(2,1)}, ...), branch_computations={%region_0.1_spmd, %region_1.3_spmd} | conditional | flops 2694316032 | bytes 64064024 | solution.py:135
  68.7 3.4 convolution_bitcast_fusion
  72.2 7.9 %fusion = f32[128,128,32,1]{1,2,3,0:T(8,128)S(1)} fusion(f32[128,32,4,128]{3,0,2,1:T(8,128)S(1)} %convolution_bitcast_fusion, bf16[32,8,32]{0,2,1:T(8,128)(2,1)S(1)} %get-tuple-element.80), kind=kOutput, calls=%fused_computation.3 | convolution fusion | flops 805306368 | bytes 10518528 | tf_op jit(solution)/shard_map/cond/branch_1_fun/trjn,rjc->tcn/dot_general | solution.py:112
  80.1 3.4 convolution_bitcast_fusion.1
  83.6 8.3 %bitcast_add_fusion = f32[128,128,32]{1,2,0:T(8,128)S(1)} fusion(f32[128,128,32,1]{1,2,3,0:T(8,128)S(1)} %fusion, f32[128,32,4,128]{3,0,2,1:T(8,128)S(1)} %convolution_bitcast_fusion.1, bf16[32,8,32]{0,2,1:T(8,128)(2,1)S(1)} %get-tuple-element.80), kind=kOutput, calls=%fused_computation.17 | convolution fusion | flops 805830656 | bytes 12615680 | tf_op jit(solution)/shard_map/cond/branch_1_fun/trjn,rjc->tcn/dot_general | solution.py:112
  91.8 3.6 fusion.7
  95.5 1.3 fusion.6
  97.1 1.4 collective-permute-start.1
  98.5 7.5 %pad_maximum_fusion = bf16[32,2,4,128,128]{4,3,2,0,1:T(8,128)(2,1)} fusion(bf16[32,1,4,128,128]{4,3,2,0,1:T(8,128)(2,1)} %bitcast.25, bf16[32,1,4,128,128]{4,3,2,0,1:T(8,128)(2,1)} %bitcast.24), kind=kLoop, calls=%fused_computation.115 | loop fusion | flops 4194304 | bytes 16777216 | tf_op jit(solution)/shard_map/stack | solution.py:80
  106.0 11.1 %copy.112 = bf16[32,2,4,128,128]{4,2,1,3,0:T(4,128)(2,1)} copy(bf16[32,2,4,128,128]{4,3,2,0,1:T(8,128)(2,1)} %pad_maximum_fusion) | data formatting | bytes 16777216 | tf_op jit(solution)/shard_map/stack | solution.py:80
  117.1 16.8 %convolution_convert_fusion = bf16[32,32,128,128]{3,1,2,0:T(8,128)(2,1)} fusion(pred[32,8,32,1]{2,1,3,0:T(8,128)(4,1)S(1)} %copy.126, bf16[32,8,128,128]{3,1,2,0:T(8,128)(2,1)} %bitcast.123), kind=kOutput, calls=%fused_computation.114 | convolution fusion | flops 285212672 | bytes 41951232 | tf_op jit(solution)/shard_map/rjkn,rjc->rkcn/dot_general | solution.py:86
  133.8 22.6 %copy.160 = bf16[512,8,32,128]{3,1,2,0:T(8,128)(2,1)} copy(bf16[512,8,32,128]{3,2,1,0:T(8,128)(2,1)} %bitcast.122) | data formatting | bytes 67108864
  156.7 2.9 conditional.9
  156.8 1.5 broadcast.316
  158.3 1.1 broadcast.317
  159.6 1.7 collective-permute-start.2
  161.4 3.7 conditional.10
  161.5 1.0 copy.173
  162.5 1.6 broadcast.320
  164.1 1.1 broadcast.321
  165.2 1.9 collective-permute-start.3
  167.2 1.3 broadcast_select_fusion.3
  168.5 1.4 select_select_fusion.3
  170.0 1.3 conditional.11
  170.2 1.1 broadcast.325
  171.3 1.3 copy-done.9
  172.6 2.2 select_select_fusion
  174.9 1.1 conditional.12
  174.9 1.1 broadcast.328
  176.0 1.6 collective-permute-start.4
  177.6 3.0 broadcast_select_fusion.2
  180.6 1.4 conditional.13
  180.6 1.1 broadcast.332
  182.0 1.6 collective-permute-start.5
  183.7 3.0 broadcast_select_fusion.1
  186.6 1.1 conditional.14
  186.6 1.1 broadcast.336
  187.7 1.3 collective-permute-start.6
  189.3 1.4 select_bitcast_fusion
  190.7 1.2 copy.142
  191.9 207.2 %collective-permute-done.6 = bf16[128,4096]{1,0:T(8,128)(2,1)} collective-permute-done((bf16[128,4096]{1,0:T(8,128)(2,1)}, bf16[128,4096]{1,0:T(8,128)(2,1)}, u32[]{:S(2)}, u32[]{:S(2)}) %collective-permute-start.6) | collective-permute-done | bytes 1048608 | tf_op jit(solution)/shard_map/ppermute | solution.py:195
  399.1 2.7 broadcast_select_fusion
  401.8 22.1 %conditional.15 = (bf16[128,4096]{1,0:T(8,128)(2,1)}, bf16[128,4096]{1,0:T(8,128)(2,1)S(1)}) conditional(s32[]{:T(128)} %convert_element_type.154, bf16[128,4096]{1,0:T(8,128)(2,1)} %broadcast_select_fusion, (bf16[128,4096]{1,0:T(8,128)(2,1)}, bf16[128,4096]{1,0:T(8,128)(2,1)S(1)}, f32[128,4096]{1,0:T(8,128)S(1)}, bf16[4096,4096]{1,0:T(8,128)(2,1)}, ...), branch_computations={%region_24.25_spmd, %region_25.28_spmd} | conditional | flops 4308598784 | bytes 56644168 | solution.py:184
  401.9 2.2 fusion.61
  404.2 16.7 %fusion.57 = (f32[128]{0:T(128)S(1)}, f32[128,4096]{1,0:T(8,128)S(1)}) fusion(bf16[128,4096]{1,0:T(8,128)(2,1)S(1)} %get-tuple-element.107, f32[128]{0:T(128)S(1)} %add_rsqrt_fusion.7, f32[4096]{0:T(1024)S(1)} %bitcast.140, bf16[128,4096]{1,0:T(8,128)(2,1)S(1)} %get-tuple-element.267, bf16[4096,4096]{1,0:T(8,128)(2,1)} %get-tuple-element.109), kind=kOutput, calls=%fused_computation.104 | convolution fusion | flops 4297588736 | bytes 37766144 | tf_op jit(solution)/shard_map/cond/branch_1_fun/dot_general | solution.py:157
  420.9 3.0 fusion.62
  424.9 0.7 copy.115
  425.5 3.1 gather_fusion.2
  428.6 6.6 %copy.119 = bf16[32,4,128,128]{2,3,1,0:T(8,128)(2,1)} copy(bf16[32,4,128,128]{3,2,1,0:T(8,128)(2,1)} %bitcast.125) | data formatting | bytes 8388608 | tf_op jit(solution)/shard_map/jit(_take)/gather | solution.py:33
  435.2 6.7 %fusion.74 = f32[32,4,128,128]{2,3,1,0:T(8,128)} fusion(bf16[32,4,128,128]{2,3,1,0:T(8,128)(2,1)} %copy.119, pred[32,4]{1,0:T(8,128)(4,1)S(1)} %get-tuple-element.224, bf16[128,32,128,1]{2,1,0,3:T(8,128)(2,1)S(1)} %bitcast.126), kind=kOutput, calls=%fused_computation.125 | convolution fusion | flops 538968064 | bytes 13631616 | tf_op jit(solution)/shard_map/trk,trjn->rjkn/dot_general | solution.py:34
  442.0 3.1 gather_fusion.1
  445.1 6.5 %copy.116 = bf16[32,4,128,128]{2,3,1,0:T(8,128)(2,1)} copy(bf16[32,4,128,128]{3,2,1,0:T(8,128)(2,1)} %bitcast.124) | data formatting | bytes 8388608 | tf_op jit(solution)/shard_map/jit(_take)/gather | solution.py:33
  451.6 3.8 collective-permute-done.7
  455.4 9.2 %bitcast_add_fusion.1 = f32[32,4,128,128]{2,3,1,0:T(8,128)} fusion(f32[32,4,128,128]{2,3,1,0:T(8,128)} %collective-permute-done.7, bf16[32,4,128,128]{2,3,1,0:T(8,128)(2,1)} %copy.116, pred[32,4]{1,0:T(8,128)(4,1)S(1)} %get-tuple-element.196, bf16[128,32,128,1]{2,1,0,3:T(8,128)(2,1)S(1)} %bitcast.127), kind=kOutput, calls=%fused_computation.116 | convolution fusion | flops 541065216 | bytes 22020224 | tf_op jit(solution)/shard_map/trk,trjn->rjkn/dot_general | solution.py:34
  464.6 31.8 %all-to-all-start.1 = ((f32[32,4,128,128]{2,3,1,0:T(8,128)}), f32[32,4,128,128]{2,3,1,0:T(8,128)}, u32[]{:S(2)}, u32[]{:S(2)}) async-start(f32[32,4,128,128]{2,3,1,0:T(8,128)} %bitcast_add_fusion.1), calls=%async_computation.1 | async-start | bytes 16777216 | tf_op jit(solution)/shard_map/all_to_all | solution.py:39
  496.5 2.4 select_select_fusion.4
  498.9 2.4 select_select_fusion.2
  501.3 132.2 %all-to-all-done.1 = f32[32,4,128,128]{2,3,1,0:T(8,128)} async-done(((f32[32,4,128,128]{2,3,1,0:T(8,128)}), f32[32,4,128,128]{2,3,1,0:T(8,128)}, u32[]{:S(2)}, u32[]{:S(2)}) %all-to-all-start.1) | async-done | bytes 8388640 | tf_op jit(solution)/shard_map/all_to_all | solution.py:39
  633.5 3.8 reduce_sum.117
  637.3 0.8 copy.121
  (70 shorter events, 4.7 us)
Async XLA Ops:
  2.6 58.1 %copy-start.15 = (s32[1,256]{1,0:T(1,128)S(1)}, s32[1,256]{1,0:T(1,128)}, u32[]{:S(2)}) copy-start(s32[1,256]{1,0:T(1,128)} %param.28) | copy-start | bytes 3076
  2.6 59.8 %copy-start.2 = (bf16[2,64,4096]{2,1,0:T(8,128)(2,1)S(1)}, bf16[2,64,4096]{2,1,0:T(8,128)(2,1)}, u32[]{:S(2)}) copy-start(bf16[2,64,4096]{2,1,0:T(8,128)(2,1)} %param.24) | copy-start | bytes 3145732
  60.1 7.5 %copy-start.12 = (f32[1,4096]{1,0:T(1,128)S(1)}, f32[1,4096]{1,0:T(1,128)}, u32[]{:S(2)}) copy-start(f32[1,4096]{1,0:T(1,128)} %param.26) | copy-start | bytes 49156
  60.1 7.5 %collective-permute-start = (bf16[32,4,128,128]{3,2,1,0:T(8,128)(2,1)}, bf16[32,4,128,128]{3,2,1,0:T(8,128)(2,1)}, u32[]{:S(2)}, u32[]{:S(2)}) collective-permute-start(bf16[32,4,128,128]{3,2,1,0:T(8,128)(2,1)} %all_to_all.10), channel_id=1, source_target_pairs={{0,1},{1,0},{2,3},{3,2},{4,5},{5,4},{6,7},{7,6},{8,9},{9,8},{10,11... | collective-permute-start | bytes 12582920 | tf_op jit(solution)/shard_map/ppermute | solution.py:47
  61.4 0.9 copy-start.13
  97.1 59.3 %collective-permute-start.1 = (bf16[128,4096]{1,0:T(8,128)(2,1)}, bf16[128,4096]{1,0:T(8,128)(2,1)S(1)}, u32[]{:S(2)}, u32[]{:S(2)}) collective-permute-start(bf16[128,4096]{1,0:T(8,128)(2,1)} %get-tuple-element.134), channel_id=1, source_target_pairs={{0,64},{1,65},{2,66},{3,67},{4,68},{5,69},{6,70},{7,71},{8,72},{9,... | collective-permute-start | bytes 3145736 | tf_op jit(solution)/shard_map/ppermute | solution.py:148
  156.7 4.6 copy-start.3
  159.6 1.7 copy-start.10
  159.6 1.7 collective-permute-start.2
  161.4 5.6 copy-start.16
  161.4 5.8 copy-start.4
  165.2 3.4 collective-permute-start.3
  171.3 1.3 copy-start.9
  171.3 3.6 copy-start
  176.0 1.6 collective-permute-start.4
  182.0 1.6 collective-permute-start.5
  186.6 2.4 copy-start.14
  187.7 211.4 %collective-permute-start.6 = (bf16[128,4096]{1,0:T(8,128)(2,1)}, bf16[128,4096]{1,0:T(8,128)(2,1)}, u32[]{:S(2)}, u32[]{:S(2)}) collective-permute-start(bf16[128,4096]{1,0:T(8,128)(2,1)} %get-tuple-element.144), channel_id=1, source_target_pairs={{64,0},{65,1},{66,2},{67,3},{68,4},{69,5},{70,6},{71,7},{72,8},{73... | collective-permute-start | bytes 3145736 | tf_op jit(solution)/shard_map/ppermute | solution.py:195
  190.7 208.4 %copy-start.5 = (bf16[2,64,4096]{2,1,0:T(8,128)(2,1)S(1)}, bf16[2,64,4096]{2,1,0:T(8,128)(2,1)}, u32[]{:S(2)}) copy-start(bf16[2,64,4096]{2,1,0:T(8,128)(2,1)} %param.25) | copy-start | bytes 3145732
  404.1 16.7 %copy-start.7 = (bf16[128,4096]{1,0:T(8,128)(2,1)}, bf16[128,4096]{1,0:T(8,128)(2,1)S(1)}, u32[]{:S(2)}) copy-start(bf16[128,4096]{1,0:T(8,128)(2,1)S(1)} %get-tuple-element.267) | copy-start | bytes 3145732 | tf_op jit(solution)/shard_map/cond
  420.9 3.0 copy-start.8
  428.6 6.6 %copy-start.6 = (bf16[16,8,32,128]{3,2,1,0:T(8,128)(2,1)S(1)}, bf16[16,8,32,128]{3,2,1,0:T(8,128)(2,1)}, u32[]{:S(2)}) copy-start(bf16[16,8,32,128]{3,2,1,0:T(8,128)(2,1)} %copy.142) | copy-start | bytes 3145732
  441.9 13.5 %collective-permute-start.7 = (f32[32,4,128,128]{2,3,1,0:T(8,128)}, f32[32,4,128,128]{2,3,1,0:T(8,128)}, u32[]{:S(2)}, u32[]{:S(2)}) collective-permute-start(f32[32,4,128,128]{2,3,1,0:T(8,128)} %fusion.74), channel_id=1, source_target_pairs={{0,1},{1,0},{2,3},{3,2},{4,5},{5,4},{6,7},{7,6},{8,9},{9,8},{10,11... | collective-permute-start | bytes 25165832 | tf_op jit(solution)/shard_map/ppermute | solution.py:37
  464.6 31.8 %copy-start.1 = (bf16[128,4096]{1,0:T(8,128)(2,1)S(1)}, bf16[128,4096]{1,0:T(8,128)(2,1)}, u32[]{:S(2)}) copy-start(bf16[128,4096]{1,0:T(8,128)(2,1)} %copy-done) | copy-start | bytes 3145732
  464.6 31.8 %copy-start.11 = (bf16[128,4096]{1,0:T(8,128)(2,1)S(1)}, bf16[128,4096]{1,0:T(8,128)(2,1)}, u32[]{:S(2)}) copy-start(bf16[128,4096]{1,0:T(8,128)(2,1)} %copy-done.10) | copy-start | bytes 3145732
  464.6 168.8 %all-to-all-start.1 = ((f32[32,4,128,128]{2,3,1,0:T(8,128)}), f32[32,4,128,128]{2,3,1,0:T(8,128)}, u32[]{:S(2)}, u32[]{:S(2)}) async-start(f32[32,4,128,128]{2,3,1,0:T(8,128)} %bitcast_add_fusion.1), calls=%async_computation.1 | async-start | bytes 16777216 | tf_op jit(solution)/shard_map/all_to_all | solution.py:39
